TPU v7x, 32 devices: a whole 2x2x4 slice. The times are simulated.
32 devices in a mesh: dp: 16 (over z, y, x), mp: 2 (over core).
Axes of the slice: x: 2, y: 2, z: 4, core: 2. Of those that a mesh axis runs over, the one named last changes fastest.
Arguments:
- tokens: bfloat16 [7168, 4544], P('dp'), may hold values from -32 to 32
- layer_norm_gain: bfloat16 [4544], replicated, may hold values from 0.5 to 1.5
- layer_norm_bias: bfloat16 [4544], replicated, may hold values from -3 to 3
- query_weight: bfloat16 [4544, 4096], P('dp', 'mp'), may hold values from -3 to 3
- key_value_weight: bfloat16 [4544, 128], P('dp'), may hold values from -3 to 3
- output_weight: bfloat16 [4096, 4544], P('dp', 'mp'), may hold values from -0.09375 to 0.09375
- adapter_down_factors: bfloat16 [16, 4544, 16], P('dp', 'mp'), may hold values from -0.09375 to 0.09375
- adapter_up_factors: bfloat16 [16, 16, 4096], P('dp', None, 'mp'), may hold values from -1.5 to 1.5
- lengths: int32 [16, 4], P('dp'), may hold values from 1 to 224, 448 in all within a row
- prompt_adapter: int32 [16, 4], P('dp'), may hold values from 0 to 15
- prompt_page_table: int32 [16, 8], P('dp'), may hold values from 0 to 7, each once within a row
- adapter_storage: int32 [16], replicated, may hold values from 0 to 15, each once
Outputs:
- attn_proj: bfloat16 [7168, 4544], P('dp', 'mp')
- kv_cache: bfloat16 [128, 128, 128], P('dp')
Inputs may be any that keep to these rules, and one draw needn't show every extreme that they name: `lengths`: each row sums to 448. `prompt_page_table`: row r lists each of the 8 pages of the pool of dp index r once; entry p * 2 + k is the page of tokens k * 128 to (k + 1) * 128 - 1 of that row's prompt p. `adapter_storage`: every storage slot holds exactly one adapter.
All inputs are finite; a program needn't handle non-finite values.
Results may differ from a plain program's by a relative error of at most 0.012.
The roundings to bfloat16 on the way count: a program that leaves them out, or rounds other values in their place, can miss the bound.
Values may be sent and summed in bfloat16 or wider, within the bound.
No kernel may reach another device: no remote copies, remote signals or barrier semaphores. Data moves between devices by JAX's collectives and lax.ppermute only.
A program may use at most 192 MiB of HBM per device.

v0:
```python
import functools
import math

import jax
import jax.numpy as jnp
from jax import lax
from jax.sharding import Mesh, PartitionSpec as P
from jax.experimental.layout import Layout, with_layout_constraint

HEAD_SIZE = 64
PAGE = 128


def pack_columns(part, shard_rows, padded_rows):
    flat = part.reshape(-1)
    width = -(-flat.shape[0] // shard_rows)
    flat = jnp.pad(flat, (0, width * shard_rows - flat.shape[0]))
    return jnp.pad(flat.reshape(shard_rows, width), ((0, padded_rows - shard_rows), (0, 0)))


def unpack_columns(block, shape, shard_rows):
    shard_count = block.shape[0]
    size = math.prod(shape)
    flat = block[:, :shard_rows, :].reshape(shard_count, -1)[:, :size]
    return flat.reshape((shard_count * shape[0],) + tuple(shape[1:]))


def pad_features(x, shard_count, padded_rows):
    rows, width = x.shape
    split = x.reshape(rows, shard_count, width // shard_count)
    split = jnp.pad(split, ((0, 0), (0, 0), (0, padded_rows - width // shard_count)))
    return split.reshape(rows, shard_count * padded_rows)


def row_major(x):
    return with_layout_constraint(x, Layout(major_to_minor=tuple(range(x.ndim))))


def layer_norm(tokens, layer_norm_gain, layer_norm_bias):
    values = tokens.astype(jnp.float32)
    row_mean = jnp.mean(values, axis=-1, keepdims=True)
    centred = values - row_mean
    row_var = jnp.mean(centred * centred, axis=-1, keepdims=True)
    scaled = centred * lax.rsqrt(row_var + 1e-05)
    return (
        scaled * layer_norm_gain.astype(jnp.float32) + layer_norm_bias.astype(jnp.float32)
    ).astype(jnp.bfloat16)


def layout(lengths_row, row_number_count):
    prompt_end = jnp.cumsum(lengths_row)
    prompt_start = prompt_end - lengths_row
    row_index = jnp.arange(row_number_count, dtype=jnp.int32)
    member = (row_index[:, None] >= prompt_start[None, :]) & (
        row_index[:, None] < prompt_end[None, :]
    )
    first_row = jnp.sum(jnp.where(member, prompt_start[None, :], 0), axis=1)
    prompt_numbers = jnp.arange(lengths_row.shape[0], dtype=jnp.int32)
    prompt_index = jnp.sum(jnp.where(member, prompt_numbers[None, :], 0), axis=1)
    position = (row_index - first_row).astype(jnp.float32)
    return (member, position, prompt_start, prompt_index)


def rotate(values, position):
    half_width = values.shape[-1] // 2
    frequency = jnp.exp(
        jnp.arange(half_width, dtype=jnp.float32) * (-math.log(10000.0) / half_width)
    )
    angles = position[:, None, None] * frequency[None, None, :]
    cosine = jnp.cos(angles)
    sine = jnp.sin(angles)
    leading = values[..., :half_width]
    trailing = values[..., half_width:]
    return jnp.concatenate(
        [leading * cosine - trailing * sine, trailing * cosine + leading * sine], axis=-1
    )


def attend(queries, keys_rot, values, prompt_index):
    row_number_count = queries.shape[0]
    head_width = queries.shape[2]
    row_index = jnp.arange(row_number_count, dtype=jnp.int32)
    allowed = (prompt_index[:, None] == prompt_index[None, :]) & (
        row_index[None, :] <= row_index[:, None]
    )
    scores = jnp.einsum("thd,sd->hts", queries, keys_rot, preferred_element_type=jnp.float32) * (
        1.0 / math.sqrt(head_width)
    )
    scores = jnp.where(allowed[None, :, :], scores, -jnp.inf)
    row_peak = jnp.max(scores, axis=-1, keepdims=True)
    weights = jnp.exp(scores - row_peak)
    probs = (weights / jnp.sum(weights, axis=-1, keepdims=True)).astype(jnp.bfloat16)
    context = jnp.einsum("hts,sd->thd", probs, values, preferred_element_type=jnp.float32)
    return context.astype(jnp.bfloat16)


def fill_pages(kv_rot, lengths_row, prompt_start, table_row, page_slots):
    page_count = table_row.shape[0]
    prompt_count = lengths_row.shape[0]
    per_prompt = page_count // prompt_count
    page_index = jnp.arange(page_count, dtype=jnp.int32)
    entry = jnp.sum(
        jnp.where(table_row[None, :] == page_index[:, None], page_index[None, :], 0), axis=1
    )
    prompt_of = entry // per_prompt
    page_of = entry % per_prompt
    prompt_numbers = jnp.arange(prompt_count, dtype=jnp.int32)
    chosen = prompt_of[:, None] == prompt_numbers[None, :]
    prompt_len = jnp.sum(jnp.where(chosen, lengths_row[None, :], 0), axis=1)
    base_row = jnp.sum(jnp.where(chosen, prompt_start[None, :], 0), axis=1)
    within = page_of[:, None] * page_slots + jnp.arange(page_slots, dtype=jnp.int32)[None, :]
    valid = within < prompt_len[:, None]
    source = jnp.minimum(base_row[:, None] + within, kv_rot.shape[0] - 1)
    return jnp.where(valid[:, :, None], kv_rot[source], jnp.zeros((), kv_rot.dtype))


def swap(x, axis_name):
    return lax.ppermute(x, axis_name, [(0, 1), (1, 0)])


def pair_join(own, other, own_slot, axis):
    first = own_slot == 0
    lower = jnp.where(first, own, other)
    upper = jnp.where(first, other, own)
    return jnp.concatenate([lower, upper], axis=axis)


def mp_gather(x, axis, mp_count):
    if mp_count == 2:
        return pair_join(x, swap(x, "mp"), lax.axis_index("mp"), axis)
    return lax.all_gather(x, "mp", axis=axis, tiled=True)


def mp_pieces(x, mp_count):
    if mp_count == 2:
        other = swap(x, "mp")
        first = lax.axis_index("mp") == 0
        return [jnp.where(first, x, other), jnp.where(first, other, x)]
    stacked = lax.all_gather(x, "mp", axis=0, tiled=False)
    return [stacked[m] for m in range(mp_count)]


def half_of(x, axis, which):
    width = x.shape[axis] // 2
    return lax.dynamic_slice_in_dim(x, which * width, width, axis)


def shards(
    tokens,
    layer_norm_gain,
    layer_norm_bias,
    query_weight,
    key_value_weight,
    output_weight,
    adapter_down_factors,
    adapter_up_factors,
    lengths,
    prompt_adapter,
    prompt_page_table,
    adapter_storage,
    mp_count,
):
    side = lax.axis_index("dl")
    mp_index = lax.axis_index("mp")
    own_rows = tokens.shape[0]
    group_count = lengths.shape[0]
    group_rows = own_rows // group_count
    prompt_count = lengths.shape[1]
    pair_rows = 2 * own_rows

    normed = layer_norm(tokens, layer_norm_gain, layer_norm_bias)

    shard_rows = query_weight.shape[0]
    rank_width = adapter_down_factors.shape[2]
    kept = (
        half_of(query_weight, 1, side),
        key_value_weight,
        adapter_down_factors,
        half_of(adapter_up_factors, 2, side),
    )
    sent = (
        half_of(query_weight, 1, 1 - side),
        key_value_weight,
        adapter_down_factors,
        half_of(adapter_up_factors, 2, 1 - side),
    )
    padded_rows = -(-shard_rows // 16) * 16
    kept_cols = [pack_columns(part, shard_rows, padded_rows) for part in kept]
    widths = [part.shape[1] for part in kept_cols]
    kept_block = jnp.concatenate(kept_cols, axis=1)
    sent_block = jnp.concatenate(
        [pack_columns(part, shard_rows, padded_rows) for part in sent], axis=1
    )
    pair_block = pair_join(kept_block[None], swap(sent_block, "dl")[None], side, 0)
    gathered = lax.all_gather(pair_block, "dh", axis=0, tiled=False)
    gathered = row_major(gathered).reshape((-1,) + gathered.shape[2:])
    shard_count = gathered.shape[0]
    offsets = [sum(widths[:i]) for i in range(len(widths))]
    unpacked = [
        unpack_columns(gathered[:, :, off : off + width], part.shape, shard_rows)
        for off, width, part in zip(offsets, widths, kept)
    ]
    _, _, down_all, up_cols = unpacked
    projection_block = gathered.reshape(-1, gathered.shape[2])

    out_kept = half_of(output_weight, 1, side)
    out_sent = half_of(output_weight, 1, 1 - side)
    out_pair = pair_join(out_kept[None], swap(out_sent, "dl")[None], side, 0)
    out_gathered = row_major(lax.all_gather(out_pair, "dh", axis=0, tiled=False))
    out_cols = out_gathered.reshape(-1, out_kept.shape[1])

    normed_padded = pad_features(normed, shard_count, padded_rows)
    row_half = own_rows // mp_count
    partner_piece = swap(
        lax.dynamic_slice_in_dim(normed_padded, mp_index * row_half, row_half, 0), "dl"
    )
    partner_normed = jnp.concatenate(mp_pieces(partner_piece, mp_count), axis=0)
    normed_pair = jnp.concatenate([normed_padded, partner_normed], axis=0)
    small = jnp.concatenate([lengths, prompt_adapter], axis=1)
    small_pair = jnp.concatenate([small, swap(small, "dl")], axis=0)
    lengths_pair = small_pair[:, :prompt_count]
    adapter_pair = small_pair[:, prompt_count:]

    member_grouped, position_grouped, start_grouped, index_grouped = jax.vmap(
        lambda one_row: layout(one_row, group_rows)
    )(lengths_pair)
    pair_groups = 2 * group_count
    pair_prompts = pair_groups * prompt_count
    own_prompts = group_count * prompt_count
    position = position_grouped.reshape(pair_rows)
    prompt_global = (
        index_grouped + (jnp.arange(pair_groups, dtype=jnp.int32) * prompt_count)[:, None]
    ).reshape(pair_rows)
    member = prompt_global[:, None] == jnp.arange(pair_prompts, dtype=jnp.int32)[None, :]

    adapter_count = adapter_storage.shape[0]
    adapter_numbers = jnp.arange(adapter_count, dtype=jnp.int32)
    adapters_flat = adapter_pair.reshape(pair_prompts)
    storage_slots = jnp.sum(
        jnp.where(adapter_numbers[None, :] == adapters_flat[:, None], adapter_storage[None, :], 0),
        axis=1,
    )
    slot_rows = down_all.shape[0]
    matches = (storage_slots[:, None] == jnp.arange(slot_rows, dtype=jnp.int32)[None, :]).astype(
        jnp.bfloat16
    )
    down_selected = jnp.einsum(
        "pn,ndr->pdr", matches[:own_prompts], down_all, preferred_element_type=jnp.float32
    ).astype(jnp.bfloat16)
    up_selected = jnp.einsum(
        "pn,nrc->prc", matches, up_cols, preferred_element_type=jnp.float32
    ).astype(jnp.bfloat16)

    feature_columns = adapter_down_factors.shape[1]
    features = lax.dynamic_slice_in_dim(normed, mp_index * feature_columns, feature_columns, 1)
    own_member = member[:own_rows, :own_prompts]
    all_ranks = jnp.dot(
        features,
        jnp.transpose(down_selected, (1, 0, 2)).reshape(feature_columns, own_prompts * rank_width),
        preferred_element_type=jnp.float32,
    ).reshape(own_rows, own_prompts, rank_width)
    rank_portion = jnp.sum(jnp.where(own_member[:, :, None], all_ranks, 0.0), axis=1)
    ranks = lax.psum(rank_portion, "mp").astype(jnp.bfloat16)
    ranks_pair = jnp.concatenate([ranks, swap(ranks, "dl")], axis=0)
    spread = jnp.where(member[:, :, None], ranks_pair[:, None, :], jnp.zeros((), jnp.bfloat16))
    adapted_queries = jnp.dot(
        spread.reshape(pair_rows, pair_prompts * rank_width),
        up_selected.reshape(pair_prompts * rank_width, -1),
        preferred_element_type=jnp.float32,
    )

    projected = jnp.dot(normed_pair, projection_block, preferred_element_type=jnp.float32)
    query_base = projected[:, : widths[0]]
    kv_base = projected[:, widths[0] : widths[0] + widths[1]]
    queries = rotate(
        (query_base + adapted_queries).reshape(pair_rows, -1, HEAD_SIZE), position
    ).astype(jnp.bfloat16)
    keys_rot = rotate(kv_base[:, None, :HEAD_SIZE], position)[:, 0, :]
    kv_rot = jnp.concatenate([keys_rot, kv_base[:, HEAD_SIZE:]], axis=1).astype(jnp.bfloat16)
    local_heads = queries.shape[1]
    queries_grouped = queries.reshape(pair_groups, group_rows, local_heads, HEAD_SIZE)
    kv_grouped = kv_rot.reshape(pair_groups, group_rows, 2 * HEAD_SIZE)
    context_grouped = jax.vmap(
        lambda q_part, kv_part, idx_part: attend(
            q_part, kv_part[:, :HEAD_SIZE], kv_part[:, HEAD_SIZE:], idx_part
        )
    )(queries_grouped, kv_grouped, index_grouped)
    context = context_grouped.reshape(pair_rows, local_heads * HEAD_SIZE)

    partner_context = swap(context, "dl")
    partner_context = jnp.concatenate(
        [partner_context[own_rows:], partner_context[:own_rows]], axis=0
    )
    chip_context = jnp.stack([context, partner_context])
    pieces = mp_pieces(chip_context, mp_count)
    block = context.shape[1]

    def project(row_start):
        total = None
        for m in range(mp_count):
            for which in range(2):
                quarter = 2 * m + jnp.where(which == 0, side, 1 - side)
                rows = lax.dynamic_slice_in_dim(out_cols, quarter * block, block, 0)
                part = jnp.dot(
                    pieces[m][which, row_start : row_start + own_rows],
                    rows,
                    preferred_element_type=jnp.float32,
                )
                total = part if total is None else total + part
        return total.astype(jnp.bfloat16)

    received_out = swap(project(own_rows), "dl")
    own_out = project(0)
    attn_proj = pair_join(own_out, received_out, side, 1)

    cache_grouped = jax.vmap(
        lambda kv_part, len_part, start_part, table_part: fill_pages(
            kv_part, len_part, start_part, table_part, PAGE
        )
    )(kv_grouped[:group_count], lengths, start_grouped[:group_count], prompt_page_table)
    kv_cache = cache_grouped.reshape(group_count * prompt_page_table.shape[1], PAGE, 2 * HEAD_SIZE)
    return (attn_proj, kv_cache)


def solution(mesh):
    dp_count = mesh.shape["dp"]
    mp_count = mesh.shape["mp"]
    pair_mesh = Mesh(
        mesh.devices.reshape(dp_count // 2, 2, mp_count), ("dh", "dl", "mp")
    )
    dp = ("dh", "dl")
    return jax.shard_map(
        functools.partial(shards, mp_count=mp_count),
        mesh=pair_mesh,
        in_specs=(
            P(dp, None),
            P(),
            P(),
            P(dp, "mp"),
            P(dp, None),
            P(dp, "mp"),
            P(dp, "mp", None),
            P(dp, None, "mp"),
            P(dp, None),
            P(dp, None),
            P(dp, None),
            P(),
        ),
        out_specs=(P(dp, "mp"), P(dp, None, None)),
        check_vma=False,
    )
```

profile of v0, /device:TPU:0, one launch (start us, length us, event | category | flops | bytes accessed | tf_op | source)
XLA Modules:
  0.0 423.1 jit_solution(11302860204537171407)
XLA Ops:
  7.3 1.4 constant_dynamic-slice_fusion.2
  9.7 3.0 collective-permute-start.2
  13.0 17.8 %collective-permute-done.2 = bf16[288,1338]{1,0:T(8,128)(2,1)S(1)} collective-permute-done((bf16[288,1338]{1,0:T(8,128)(2,1)S(1)}, bf16[288,1338]{1,0:T(8,128)(2,1)S(1)}, u32[]{:S(2)}, u32[]{:S(2)}) %collective-permute-start.2) | collective-permute-done | bytes 770720 | tf_op jit(solution)/shard_map/ppermute | solution.py:118
  31.2 1.4 pad_maximum_fusion.3
  32.7 3.0 convert_reduce_fusion
  36.0 1.2 fusion.8
  37.3 4.2 fusion.11
  41.5 11.5 %reshape.682 = bf16[448,16,284]{2,1,0:T(8,128)(2,1)} reshape(bf16[448,4544]{1,0:T(8,128)(2,1)} %fusion.11) | data formatting | bytes 8142848 | tf_op jit(solution)/shard_map/reshape | solution.py:30
  53.0 8.4 %copy.100 = bf16[448,16,284]{0,2,1:T(8,128)(2,1)} copy(bf16[448,16,284]{2,1,0:T(8,128)(2,1)} %reshape.682) | data formatting | bytes 8142848 | tf_op jit(solution)/shard_map/reshape | solution.py:30
  61.4 5.3 %pad.34 = bf16[448,16,288]{0,2,1:T(8,128)(2,1)} pad(bf16[448,16,284]{0,2,1:T(8,128)(2,1)} %copy.100, bf16[]{:T(256)} %constant.33.clone.1), padding=0_0x0_0x0_4 | pad | bytes 8200194 | tf_op jit(solution)/shard_map/jit(_pad)/pad | solution.py:31
  66.6 3.2 constant_dynamic-slice_fusion.3
  69.9 2.4 copy.76
  72.3 1.8 collective-permute-start
  74.4 1.8 collective-permute-start.7
  76.4 44.0 %collective-permute-done.3 = s32[1,8]{1,0:T(1,128)S(1)} collective-permute-done((s32[1,8]{1,0:T(1,128)S(1)}, s32[1,8]{1,0:T(1,128)S(1)}, u32[]{:S(2)}, u32[]{:S(2)}) %collective-permute-start.3) | collective-permute-done | bytes 64 | tf_op jit(solution)/shard_map/ppermute | solution.py:118
  122.3 1.2 multiply_cosine_fusion
  123.5 1.2 compare_and_fusion
  124.7 6.4 %collective-permute-done.7 = bf16[256,1136]{0,1:T(8,128)(2,1)S(1)} collective-permute-done((bf16[256,1136]{0,1:T(8,128)(2,1)S(1)}, bf16[256,1136]{0,1:T(8,128)(2,1)S(1)}, u32[]{:S(2)}, u32[]{:S(2)}) %collective-permute-start.7) | collective-permute-done | bytes 581664 | tf_op jit(solution)/shard_map/ppermute | solution.py:118
  131.3 1.1 pad_maximum_fusion.10
  132.5 2.8 copy.77
  135.3 4.1 copy.78
  139.4 4.1 broadcast_select_fusion.3
  143.6 71.5 %all-gather.5.cloned.1.call-done = bf16[16,288,1338]{2,1,0:T(8,128)(2,1)} async-done(((bf16[2,288,1338]{2,1,0:T(8,128)(2,1)}), bf16[16,288,1338]{2,1,0:T(8,128)(2,1)}) %all-gather.5.cloned.1.call-update) | async-done | bytes 12331024 | tf_op jit(solution)/shard_map/all_gather | solution.py:195
  215.1 1.3 slice.125
  216.4 8.0 %reshape_reshape.7 = bf16[16,2272,16]{2,1,0:T(8,128)(2,1)} reshape(bf16[16,284,128]{2,1,0:T(8,128)(2,1)S(1)} %slice.125) | data formatting | bytes 2326528 | tf_op jit(solution)/shard_map/reshape;reshape | solution.py:25
  224.4 7.7 %copy.82 = bf16[16,2272,16]{1,0,2:T(8,128)(2,1)S(1)} copy(bf16[16,2272,16]{2,1,0:T(8,128)(2,1)} %reshape_reshape.7) | data formatting | bytes 2326528 | tf_op jit(solution)/shard_map/reshape;reshape | solution.py:25
  232.4 2.6 fusion.56
  235.1 3.4 psum.7
  238.5 1.5 collective-permute-start.4
  240.0 1.4 slice.126
  241.4 2.6 reshape.659
  244.0 19.4 %fusion.12 = f32[896,1338]{0,1:T(8,128)S(1)} fusion(bf16[4608,1338]{1,0:T(8,128)(2,1)} %bitcast.138, bf16[224,4608]{0,1:T(8,128)(2,1)} %get-tuple-element.9, bf16[224,4608]{0,1:T(8,128)(2,1)S(1)} %copy-done.5, bf16[448,4608]{0,1:T(8,128)(2,1)} %bitcast.135), kind=kOutput, calls=%fused_computation.18 | convolution fusion | flops 11073355776 | bytes 25383936 | tf_op jit(solution)/shard_map/dot_general | solution.py:272
  264.3 1.3 copy-done.4
  265.9 0.8 pad_maximum_fusion.12
  266.8 2.8 slice_add_fusion
  270.1 0.9 concatenate.62
  271.2 0.9 concatenate.63
  272.1 1.2 copy.88
  273.3 16.3 %fusion.114 = (f32[2,16,448]{2,1,0:T(8,128)S(1)}, f32[2,16,448,448]{2,3,1,0:T(8,128)}) fusion(pred[2,448,448]{1,2,0:T(8,128)(4,1)} %compare_and_fusion, bf16[2,448,16,32]{1,3,2,0:T(8,128)(2,1)} %copy.88, bf16[2,448,16,32]{1,3,2,0:T(8,128)(2,1)S(1)} %copy.87, bf16[2,448,64,1]{1,0,2,3:T(2,128)(2,1)S(1)} %bitcast.142), kind=kOutput, calls=%fused_computation.200 | convolution fusion | flops 851444160 | bytes 28098560 | tf_op jit(solution)/shard_map/vmap()/sub | solution.py:91
  289.6 13.3 %convert_bitcast_fusion = bf16[2,448,16,64]{1,3,2,0:T(8,128)(2,1)} fusion(f32[2,16,448,448]{2,3,1,0:T(8,128)} %get-tuple-element.33, f32[2,16,448]{2,1,0:T(8,128)S(1)} %get-tuple-element.32, bf16[2,448,64,1]{1,0,2,3:T(2,128)(2,1)S(1)} %bitcast.141), kind=kOutput, calls=%fused_computation.46 | convolution fusion | flops 835846144 | bytes 27697152 | tf_op jit(solution)/shard_map/vmap(hts,sd->thd)/dot_general | solution.py:93
  302.9 3.8 copy.92
  306.7 2.6 reshape.662
  309.2 0.7 collective-permute-start.5
  309.9 2.5 stack_reshape.3
  312.4 39.1 %collective-permute-done.5 = bf16[896,1024]{0,1:T(8,128)(2,1)} collective-permute-done((bf16[896,1024]{0,1:T(8,128)(2,1)}, bf16[896,1024]{0,1:T(8,128)(2,1)}, u32[]{:S(2)}, u32[]{:S(2)}) %collective-permute-start.5) | collective-permute-done | bytes 1835040 | tf_op jit(solution)/shard_map/ppermute | solution.py:118
  351.5 2.0 fusion.112
  354.2 0.9 copy-done.2
  355.1 2.5 pad_maximum_fusion
  358.0 12.6 %copy.94 = bf16[16,256,1136]{2,1,0:T(8,128)(2,1)} copy(bf16[16,256,1136]{1,2,0:T(8,128)(2,1)} %all-gather.7.cloned.1.call-done) | data formatting | bytes 18612224 | tf_op jit(solution)/shard_map/all_gather | solution.py:209
  370.8 4.5 %gather_fusion = bf16[1024,128]{1,0:T(8,128)(2,1)S(1)} fusion(bf16[1,448,128]{2,1,0:T(8,128)(2,1)S(1)} %copy.95, s32[1024]{0:T(1024)S(1)} %fusion.89), kind=kCustom, calls=%fused_computation | custom fusion | bytes 532480 | tf_op jit(solution)/shard_map/vmap()/gather | solution.py:114
  375.4 3.4 broadcast_select_fusion.1
  378.8 1.9 copy-done.1
  380.7 1.6 fusion.31
  382.3 1.6 fusion.27
  383.9 1.6 fusion.35
  385.5 1.5 fusion.24
  387.1 0.9 collective-permute-start.8
  388.0 0.9 broadcast_select_fusion.6
  388.9 1.4 fusion.37
  390.3 1.4 fusion.33
  391.7 1.4 fusion.29
  393.1 19.3 %collective-permute-done.8 = bf16[448,1136]{1,0:T(8,128)(2,1)S(1)} collective-permute-done((bf16[448,1136]{1,0:T(8,128)(2,1)S(1)}, bf16[448,1136]{1,0:T(8,128)(2,1)S(1)}, u32[]{:S(2)}, u32[]{:S(2)}) %collective-permute-start.8) | collective-permute-done | bytes 1017888 | tf_op jit(solution)/shard_map/ppermute | solution.py:118
  412.4 1.6 broadcast_select_fusion.5
  414.0 1.8 pad_maximum_fusion.2
  (125 shorter events, 8.2 us)
Async XLA Ops:
  7.2 1.5 copy-start.11
  7.2 1.7 copy-start.10
  7.2 2.4 copy-start.9
  7.2 207.9 %all-gather.5.cloned.1.call-start = ((), (), s32[]{:S(2)}) async-start(), calls=%async_computation | async-start | bytes 14598144 | tf_op jit(solution)/shard_map/all_gather | solution.py:195
  9.7 21.1 %collective-permute-start.2 = (bf16[288,1338]{1,0:T(8,128)(2,1)S(1)}, bf16[288,1338]{1,0:T(8,128)(2,1)S(1)}, u32[]{:S(2)}, u32[]{:S(2)}) collective-permute-start(bf16[288,1338]{1,0:T(8,128)(2,1)S(1)} %fusion.64), channel_id=1, source_target_pairs={{0,2},{2,0},{1,3},{3,1},{4,6},{6,4},{5,7},{7,5},{8,10},{10,8},{9,1... | collective-permute-start | bytes 2312072 | tf_op jit(solution)/shard_map/ppermute | solution.py:118
  31.1 1.5 copy-start.16
  31.1 1.5 copy-start.17
  32.5 325.5 %all-gather.7.cloned.1.call-start = ((), (), s32[]{:S(2)}) async-start(), calls=%async_computation.1 | async-start | bytes 10469376 | tf_op jit(solution)/shard_map/all_gather | solution.py:209
  32.6 3.4 copy-start
  69.9 4.2 copy-start.22
  69.9 4.2 copy-start.24
  69.9 4.5 %copy-start.6 = (bf16[256,2272]{0,1:T(8,128)(2,1)S(1)}, bf16[256,2272]{0,1:T(8,128)(2,1)}, u32[]{:S(2)}) copy-start(bf16[256,2272]{0,1:T(8,128)(2,1)} %param.17) | copy-start | bytes 3489796
  69.9 51.6 %copy-start.27 = (s32[16]{0:T(128)S(1)}, s32[16]{0:T(128)}, u32[]{:S(2)}) copy-start(s32[16]{0:T(128)} %param.23) | copy-start | bytes 196
  72.3 48.6 %collective-permute-start = (bf16[224,4608]{1,0:T(8,128)(2,1)}, bf16[224,4608]{1,0:T(8,128)(2,1)}, u32[]{:S(2)}, u32[]{:S(2)}) collective-permute-start(bf16[224,4608]{1,0:T(8,128)(2,1)} %copy.76), channel_id=1, source_target_pairs={{0,2},{2,0},{1,3},{3,1},{4,6},{6,4},{5,7},{7,5},{8,10},{10,8},{9,1... | collective-permute-start | bytes 6193160 | tf_op jit(solution)/shard_map/ppermute | solution.py:118
  74.1 46.3 %collective-permute-start.3 = (s32[1,8]{1,0:T(1,128)S(1)}, s32[1,8]{1,0:T(1,128)S(1)}, u32[]{:S(2)}, u32[]{:S(2)}) collective-permute-start(s32[1,8]{1,0:T(1,128)S(1)} %pad_add_fusion.1), channel_id=1, source_target_pairs={{0,2},{2,0},{1,3},{3,1},{4,6},{6,4},{5,7},{7,5},{8,10},{10,8},{9,1... | collective-permute-start | bytes 104 | tf_op jit(solution)/shard_map/ppermute | solution.py:118
  74.4 56.6 %collective-permute-start.7 = (bf16[256,1136]{0,1:T(8,128)(2,1)S(1)}, bf16[256,1136]{0,1:T(8,128)(2,1)S(1)}, u32[]{:S(2)}, u32[]{:S(2)}) collective-permute-start(bf16[256,1136]{0,1:T(8,128)(2,1)S(1)} %constant_dynamic-slice_fusion), channel_id=1, source_target_pairs={{0,2},{2,0},{1,3},{3,1},{4,6},{6,4},{5,7},{7,5},{8,10},{10,8},{9,1... | collective-permute-start | bytes 1744904 | tf_op jit(solution)/shard_map/ppermute | solution.py:118
  76.3 56.2 %copy-start.20 = (f32[32]{0:T(128)}, f32[32]{0:T(128)S(1)}, u32[]{:S(2)}) copy-start(f32[32]{0:T(128)S(1)} %multiply_exponential_fusion) | copy-start | bytes 388
  120.7 0.6 copy-start.18
  120.9 14.4 %collective-permute-start.1 = (bf16[224,4608]{1,0:T(8,128)(2,1)}, bf16[224,4608]{1,0:T(8,128)(2,1)}, u32[]{:S(2)}, u32[]{:S(2)}) collective-permute-start(bf16[224,4608]{1,0:T(8,128)(2,1)} %collective-permute-done), channel_id=1, source_target_pairs={{0,1},{1,0},{2,3},{3,2},{4,5},{5,4},{6,7},{7,6},{8,9},{9,8},{10,11... | collective-permute-start | bytes 6193160 | tf_op jit(solution)/shard_map/ppermute | solution.py:118
  121.7 0.6 copy-start.25
  121.7 10.8 %copy-start.12 = (pred[896,8]{0,1:T(8,128)(4,1)}, pred[896,8]{0,1:T(8,128)(4,1)S(1)}, u32[]{:S(2)}) copy-start(pred[896,8]{0,1:T(8,128)(4,1)S(1)} %iota_compare_fusion.7) | copy-start | bytes 21508
  122.3 10.2 %copy-start.14 = (f32[896]{0:T(1024)}, f32[896]{0:T(1024)S(1)}, u32[]{:S(2)}) copy-start(f32[896]{0:T(1024)S(1)} %convert_element_type.76) | copy-start | bytes 10756
  238.5 5.5 %copy-start.5 = (bf16[224,4608]{0,1:T(8,128)(2,1)S(1)}, bf16[224,4608]{0,1:T(8,128)(2,1)}, u32[]{:S(2)}) copy-start(bf16[224,4608]{0,1:T(8,128)(2,1)} %get-tuple-element.8) | copy-start | bytes 6193156
  238.5 27.5 %collective-permute-start.4 = (bf16[448,16]{0,1:T(8,128)(2,1)S(1)}, bf16[448,16]{0,1:T(8,128)(2,1)}, u32[]{:S(2)}, u32[]{:S(2)}) collective-permute-start(bf16[448,16]{0,1:T(8,128)(2,1)S(1)} %psum.7), channel_id=1, source_target_pairs={{0,2},{2,0},{1,3},{3,1},{4,6},{6,4},{5,7},{7,5},{8,10},{10,8},{9,1... | collective-permute-start | bytes 43016 | tf_op jit(solution)/shard_map/ppermute | solution.py:118
  244.0 19.5 %copy-start.15 = (f32[896]{0:T(1024)S(1)}, f32[896]{0:T(1024)}, u32[]{:S(2)}) copy-start(f32[896]{0:T(1024)} %copy-done.14) | copy-start | bytes 10756
  244.0 19.5 %copy-start.21 = (f32[32]{0:T(128)S(1)}, f32[32]{0:T(128)}, u32[]{:S(2)}) copy-start(f32[32]{0:T(128)} %copy-done.20) | copy-start | bytes 388
  244.0 20.0 %slice-start = ((bf16[16,16472]{1,0:T(8,128)(2,1)}), bf16[16,16384]{1,0:T(8,128)(2,1)S(1)}, s32[]{:S(2)}) async-start(bf16[16,16472]{1,0:T(8,128)(2,1)} %reshape.659), calls=%async_computation.2 | async-start | bytes 1048576 | tf_op jit(solution)/shard_map/slice | solution.py:24
  244.0 20.0 %copy-start.26 = (s32[8]{0:T(128)S(1)}, s32[8]{0:T(128)}, u32[]{:S(2)}) copy-start(s32[8]{0:T(128)} %copy-done.25) | copy-start | bytes 100
  263.4 2.2 copy-start.4
  263.4 3.3 copy-start.13
  266.7 2.8 copy-start.7
  266.8 2.8 copy-start.8
  309.2 42.3 %collective-permute-start.5 = (bf16[896,1024]{0,1:T(8,128)(2,1)}, bf16[896,1024]{0,1:T(8,128)(2,1)}, u32[]{:S(2)}, u32[]{:S(2)}) collective-permute-start(bf16[896,1024]{0,1:T(8,128)(2,1)} %reshape.662), channel_id=1, source_target_pairs={{0,2},{2,0},{1,3},{3,1},{4,6},{6,4},{5,7},{7,5},{8,10},{10,8},{9,1... | collective-permute-start | bytes 5505032 | tf_op jit(solution)/shard_map/ppermute | solution.py:118
  353.6 1.5 copy-start.2
  355.1 2.5 copy-start.3
  355.1 2.5 copy-start.28
  355.1 2.7 copy-start.19
  355.1 2.7 copy-start.23
  357.6 17.8 %collective-permute-start.6 = (bf16[2,896,1024]{1,2,0:T(8,128)(2,1)}, bf16[2,896,1024]{1,2,0:T(8,128)(2,1)}, u32[]{:S(2)}, u32[]{:S(2)}) collective-permute-start(bf16[2,896,1024]{1,2,0:T(8,128)(2,1)} %pad_maximum_fusion), channel_id=1, source_target_pairs={{0,1},{1,0},{2,3},{3,2},{4,5},{5,4},{6,7},{7,6},{8,9},{9,8},{10,11... | collective-permute-start | bytes 11010056 | tf_op jit(solution)/shard_map/ppermute | solution.py:118
  375.4 5.3 %copy-start.1 = (bf16[16,256,1136]{2,1,0:T(8,128)(2,1)S(1)}, bf16[16,256,1136]{2,1,0:T(8,128)(2,1)}, u32[]{:S(2)}) copy-start(bf16[16,256,1136]{2,1,0:T(8,128)(2,1)} %copy.94) | copy-start | bytes 27918340
  387.1 25.3 %collective-permute-start.8 = (bf16[448,1136]{1,0:T(8,128)(2,1)S(1)}, bf16[448,1136]{1,0:T(8,128)(2,1)S(1)}, u32[]{:S(2)}, u32[]{:S(2)}) collective-permute-start(bf16[448,1136]{1,0:T(8,128)(2,1)S(1)} %fusion.24), channel_id=1, source_target_pairs={{0,2},{2,0},{1,3},{3,1},{4,6},{6,4},{5,7},{7,5},{8,10},{10,8},{9,1... | collective-permute-start | bytes 3053576 | tf_op jit(solution)/shard_map/ppermute | solution.py:118
Sparse Core Ops, SparseCore 0:
  32.7 182.3 all-gather.4
  217.3 133.8 all-gather.6
where the time goes:
time: 429 us; the launch traced here: 423 us
  waiting for transfers between devices  198 us (46%)
  local copies, waits for them, and re-layouts  98.4 us (23%)
  matrix products  67.2 us (16%)
  other arithmetic  30.5 us (7%)
  between operations  15.2 us (4%)
  starting transfers between devices  10.1 us (2%)
    ppermute x9, waiting for transfers between devices, swap(): return lax.ppermute(x, axis_name, [(0, 1), (1, 0)])  127 us
    all_gather x1, waiting for transfers between devices, shards(): gathered = lax.all_gather(pair_block, 'dh', axis=0, tiled=False)  71.5 us
    reshape x2, local copies, waits for them, and re-layouts, pad_features(): split = x.reshape(rows, shard_count, width // shard_count)  19.9 us
    dot_general x1, matrix products, shards(): jnp.dot(normed_pair, projection_block, preferred_element_type=jnp.float32)  19.4 us
    sub x1, matrix products, attend(): weights = jnp.exp(scores - row_peak)  16.3 us
    another operation x2, local copies, waits for them, and re-layouts, unpack_columns(): return flat.reshape((shard_count * shape[0],) + tuple(shape[1:]))  15.6 us
    dot_general x1, matrix products, attend(): jnp.einsum('hts,sd->thd', probs, values, preferred_element_type=jnp.float32)  13.3 us
    all_gather x1, local copies, waits for them, and re-layouts, shards(): lax.all_gather(out_pair, 'dh', axis=0, tiled=False)  12.6 us
  transfers between devices with their start and end apart: 11, of which 6 were waited for; matrix products, arithmetic and copies ran while one was open for 41% of the time, Pallas kernels for 0%

commit v1 on v0

--- a/solution.py
+++ b/solution.py
@@ -172,16 +172,17 @@
 
     shard_rows = query_weight.shape[0]
     rank_width = adapter_down_factors.shape[2]
+    down_by_rank = jnp.swapaxes(adapter_down_factors, 1, 2)
     kept = (
         half_of(query_weight, 1, side),
         key_value_weight,
-        adapter_down_factors,
+        down_by_rank,
         half_of(adapter_up_factors, 2, side),
     )
     sent = (
         half_of(query_weight, 1, 1 - side),
         key_value_weight,
-        adapter_down_factors,
+        down_by_rank,
         half_of(adapter_up_factors, 2, 1 - side),
     )
     padded_rows = -(-shard_rows // 16) * 16
@@ -206,8 +207,8 @@
     out_kept = half_of(output_weight, 1, side)
     out_sent = half_of(output_weight, 1, 1 - side)
     out_pair = pair_join(out_kept[None], swap(out_sent, "dl")[None], side, 0)
-    out_gathered = row_major(lax.all_gather(out_pair, "dh", axis=0, tiled=False))
-    out_cols = out_gathered.reshape(-1, out_kept.shape[1])
+    out_gathered = lax.all_gather(out_pair, "dh", axis=0, tiled=False)
+    heads_per_block = out_gathered.shape[0] * out_gathered.shape[1] // (2 * mp_count)
 
     normed_padded = pad_features(normed, shard_count, padded_rows)
     row_half = own_rows // mp_count
@@ -245,7 +246,7 @@
         jnp.bfloat16
     )
     down_selected = jnp.einsum(
-        "pn,ndr->pdr", matches[:own_prompts], down_all, preferred_element_type=jnp.float32
+        "pn,nrd->prd", matches[:own_prompts], down_all, preferred_element_type=jnp.float32
     ).astype(jnp.bfloat16)
     up_selected = jnp.einsum(
         "pn,nrc->prc", matches, up_cols, preferred_element_type=jnp.float32
@@ -254,9 +255,10 @@
     feature_columns = adapter_down_factors.shape[1]
     features = lax.dynamic_slice_in_dim(normed, mp_index * feature_columns, feature_columns, 1)
     own_member = member[:own_rows, :own_prompts]
-    all_ranks = jnp.dot(
+    all_ranks = jnp.einsum(
+        "tf,qf->tq",
         features,
-        jnp.transpose(down_selected, (1, 0, 2)).reshape(feature_columns, own_prompts * rank_width),
+        down_selected.reshape(own_prompts * rank_width, feature_columns),
         preferred_element_type=jnp.float32,
     ).reshape(own_rows, own_prompts, rank_width)
     rank_portion = jnp.sum(jnp.where(own_member[:, :, None], all_ranks, 0.0), axis=1)
@@ -291,22 +293,34 @@
     partner_context = jnp.concatenate(
         [partner_context[own_rows:], partner_context[:own_rows]], axis=0
     )
-    chip_context = jnp.stack([context, partner_context])
-    pieces = mp_pieces(chip_context, mp_count)
     block = context.shape[1]
+    if mp_count == 2:
+        other_mp = 1 - mp_index
+        pieces = [
+            (context, 2 * mp_index + side),
+            (swap(context, "mp"), 2 * other_mp + side),
+            (partner_context, 2 * mp_index + 1 - side),
+            (swap(partner_context, "mp"), 2 * other_mp + 1 - side),
+        ]
+    else:
+        stacked = lax.all_gather(jnp.stack([context, partner_context]), "mp", axis=0, tiled=False)
+        pieces = [
+            (stacked[m, which], 2 * m + jnp.where(which == 0, side, 1 - side))
+            for which in range(2)
+            for m in range(mp_count)
+        ]
 
     def project(row_start):
         total = None
-        for m in range(mp_count):
-            for which in range(2):
-                quarter = 2 * m + jnp.where(which == 0, side, 1 - side)
-                rows = lax.dynamic_slice_in_dim(out_cols, quarter * block, block, 0)
-                part = jnp.dot(
-                    pieces[m][which, row_start : row_start + own_rows],
-                    rows,
-                    preferred_element_type=jnp.float32,
-                )
-                total = part if total is None else total + part
+        for piece, quarter in pieces:
+            rows = lax.dynamic_slice_in_dim(out_gathered, quarter * (heads_per_block // 2), heads_per_block // 2, 0)
+            part = jnp.einsum(
+                "tabk,abkn->tn",
+                piece[row_start : row_start + own_rows].reshape((own_rows,) + rows.shape[:3]),
+                rows,
+                preferred_element_type=jnp.float32,
+            )
+            total = part if total is None else total + part
         return total.astype(jnp.bfloat16)
 
     received_out = swap(project(own_rows), "dl")

time: 429 us -> 404 us (0.942)
  local copies, waits for them, and re-layouts: 98.4 us -> 75.3 us
  other arithmetic: 30.5 us -> 26 us
    another operation x2 -> x1, local copies, waits for them, and re-layouts: 15.6 us -> 1.8 us  [unpack_columns(): return flat.reshape((shard_count * shape[0],) + tuple(shape[1:]))]
    all_gather x1 -> x0, local copies, waits for them, and re-layouts: 12.6 us -> none  [shards(): lax.all_gather(out_pair, 'dh', axis=0, tiled=False)]
    slice x0 -> x3, local copies, waits for them, and re-layouts: none -> 5.55 us  [project(): piece[row_start:row_start + own_rows].reshape((own_rows,) + rows.shape[:3])]
    ppermute x9 -> x10, waiting for transfers between devices: 127 us -> 128 us  [swap(): return lax.ppermute(x, axis_name, [(0, 1), (1, 0)])]
    ppermute x9 -> x10, starting transfers between devices: 10.1 us -> 11 us  [swap(): return lax.ppermute(x, axis_name, [(0, 1), (1, 0)])]
  transfers between devices with their start and end apart: 11 -> 12, of which waited for: 6 -> 7; matrix products, arithmetic and copies ran while one was open for 41% -> 39% of each run, Pallas kernels for 0% -> 0%
where the time goes in v1:
time: 404 us; the launch traced here: 399 us
  waiting for transfers between devices  199 us (49%)
  local copies, waits for them, and re-layouts  75.3 us (19%)
  matrix products  69.1 us (17%)
  other arithmetic  26 us (6%)
  between operations  14.9 us (4%)
  starting transfers between devices  11.1 us (3%)
    ppermute x10, waiting for transfers between devices, swap(): return lax.ppermute(x, axis_name, [(0, 1), (1, 0)])  128 us
    all_gather x1, waiting for transfers between devices, shards(): gathered = lax.all_gather(pair_block, 'dh', axis=0, tiled=False)  71.3 us
    reshape x2, local copies, waits for them, and re-layouts, pad_features(): split = x.reshape(rows, shard_count, width // shard_count)  19.9 us
    dot_general x1, matrix products, shards(): jnp.dot(normed_pair, projection_block, preferred_element_type=jnp.float32)  19.4 us
    sub x1, matrix products, attend(): weights = jnp.exp(scores - row_peak)  16.7 us
    dot_general x8, matrix products, project(): jnp.einsum('tabk,abkn->tn', piece[row_start:row_start + own_rows].reshape...  14.7 us
    dot_general x1, matrix products, attend(): jnp.einsum('hts,sd->thd', probs, values, preferred_element_type=jnp.float32)  12.1 us
    ppermute x10, starting transfers between devices, swap(): return lax.ppermute(x, axis_name, [(0, 1), (1, 0)])  11 us
  transfers between devices with their start and end apart: 12, of which 7 were waited for; matrix products, arithmetic and copies ran while one was open for 39% of the time, Pallas kernels for 0%

profile of v1, /device:TPU:0, one launch (start us, length us, event | category | flops | bytes accessed | tf_op | source)
XLA Modules:
  0.0 398.9 jit_solution(16957361629296004292)
XLA Ops:
  7.2 1.4 constant_dynamic-slice_fusion.2
  9.1 3.0 collective-permute-start.2
  12.4 17.8 %collective-permute-done.2 = bf16[288,1338]{1,0:T(8,128)(2,1)S(1)} collective-permute-done((bf16[288,1338]{1,0:T(8,128)(2,1)S(1)}, bf16[288,1338]{1,0:T(8,128)(2,1)S(1)}, u32[]{:S(2)}, u32[]{:S(2)}) %collective-permute-start.2) | collective-permute-done | bytes 770720 | tf_op jit(solution)/shard_map/ppermute | solution.py:118
  30.6 1.4 pad_maximum_fusion.3
  32.1 3.0 convert_reduce_fusion
  35.5 1.2 fusion.8
  36.7 4.3 %fusion.11 = bf16[448,4544]{1,0:T(8,128)(2,1)} fusion(bf16[448,4544]{1,0:T(8,128)(2,1)S(1)} %copy-done, f32[4544]{0:T(1024)S(1)} %convert_element_type.69, f32[4544]{0:T(1024)S(1)} %convert_element_type.68, f32[448]{0:T(512)S(1)} %add_rsqrt_fusion, f32[448]{0:T(512)S(1)} %broadcast_multiply_fusion), kind=kLoop, calls=%fused_computation.17 | loop fusion | flops 12214272 | bytes 8182784 | tf_op jit(solution)/shard_map/convert_element_type | solution.py:47
  41.0 11.5 %reshape.720 = bf16[448,16,284]{2,1,0:T(8,128)(2,1)} reshape(bf16[448,4544]{1,0:T(8,128)(2,1)} %fusion.11) | data formatting | bytes 8142848 | tf_op jit(solution)/shard_map/reshape | solution.py:30
  52.5 8.4 %copy.153 = bf16[448,16,284]{0,2,1:T(8,128)(2,1)} copy(bf16[448,16,284]{2,1,0:T(8,128)(2,1)} %reshape.720) | data formatting | bytes 8142848 | tf_op jit(solution)/shard_map/reshape | solution.py:30
  60.9 5.2 %pad.34 = bf16[448,16,288]{0,2,1:T(8,128)(2,1)} pad(bf16[448,16,284]{0,2,1:T(8,128)(2,1)} %copy.153, bf16[]{:T(256)} %constant.32.clone.1), padding=0_0x0_0x0_4 | pad | bytes 8200194 | tf_op jit(solution)/shard_map/jit(_pad)/pad | solution.py:31
  66.2 3.2 constant_dynamic-slice_fusion.3
  69.4 2.4 copy.108
  71.8 1.8 collective-permute-start
  74.0 1.8 collective-permute-start.5
  75.9 44.0 %collective-permute-done.3 = s32[1,8]{1,0:T(1,128)S(1)} collective-permute-done((s32[1,8]{1,0:T(1,128)S(1)}, s32[1,8]{1,0:T(1,128)S(1)}, u32[]{:S(2)}, u32[]{:S(2)}) %collective-permute-start.3) | collective-permute-done | bytes 64 | tf_op jit(solution)/shard_map/ppermute | solution.py:118
  121.4 1.2 multiply_cosine_fusion
  122.5 1.2 compare_and_fusion
  123.7 6.9 %collective-permute-done.5 = bf16[256,1136]{0,1:T(8,128)(2,1)S(1)} collective-permute-done((bf16[256,1136]{0,1:T(8,128)(2,1)S(1)}, bf16[256,1136]{0,1:T(8,128)(2,1)S(1)}, u32[]{:S(2)}, u32[]{:S(2)}) %collective-permute-start.5) | collective-permute-done | bytes 581664 | tf_op jit(solution)/shard_map/ppermute | solution.py:118
  130.9 1.2 pad_maximum_fusion.10
  132.2 2.8 copy.109
  135.0 4.2 %copy.110 = bf16[224,4608]{0,1:T(8,128)(2,1)} copy(bf16[224,4608]{1,0:T(8,128)(2,1)} %collective-permute-done.1) | data formatting | bytes 4128768 | tf_op jit(solution)/shard_map/ppermute | solution.py:118
  139.1 4.1 %broadcast_select_fusion.1 = (bf16[224,4608]{0,1:T(8,128)(2,1)}, bf16[224,4608]{0,1:T(8,128)(2,1)}) fusion(bf16[224,4608]{0,1:T(8,128)(2,1)S(1)} %copy.109, bf16[224,4608]{0,1:T(8,128)(2,1)} %copy.110, pred[]{:T(512)S(6)} %eq.121), kind=kLoop, calls=%fused_computation.48 | loop fusion | flops 2064384 | bytes 8257537 | tf_op jit(solution)/shard_map/jit(_where)/select_n | solution.py:138
  143.3 71.3 %all-gather.5.cloned.1.call-done = bf16[16,288,1338]{2,1,0:T(8,128)(2,1)} async-done(((bf16[2,288,1338]{2,1,0:T(8,128)(2,1)}), bf16[16,288,1338]{2,1,0:T(8,128)(2,1)}) %all-gather.5.cloned.1.call-update) | async-done | bytes 12331024 | tf_op jit(solution)/shard_map/all_gather | solution.py:196
  214.5 1.3 slice.119
  215.9 1.8 reshape_reshape.7
  218.2 2.6 fusion.52
  220.8 3.4 psum.7
  224.2 1.5 collective-permute-start.4
  225.8 1.3 slice.120
  227.1 2.6 reshape.682
  229.8 19.4 %fusion.12 = f32[896,1338]{0,1:T(8,128)S(1)} fusion(bf16[4608,1338]{1,0:T(8,128)(2,1)} %bitcast.169, bf16[224,4608]{0,1:T(8,128)(2,1)} %get-tuple-element.7, bf16[224,4608]{0,1:T(8,128)(2,1)S(1)} %copy-done.4, bf16[448,4608]{0,1:T(8,128)(2,1)} %bitcast.151), kind=kOutput, calls=%fused_computation.18 | convolution fusion | flops 11073355776 | bytes 25383936 | tf_op jit(solution)/shard_map/dot_general | solution.py:274
  249.2 0.5 fusion.77
  250.0 1.3 copy-done.3
  251.5 0.8 concatenate.56
  252.3 0.8 pad_maximum_fusion.12
  253.1 2.8 slice_add_fusion
  256.0 0.6 subtract_convert_fusion
  256.6 0.9 concatenate.62
  257.6 0.9 concatenate.63
  258.5 1.2 copy.119
  259.7 16.7 %fusion.112 = (f32[2,16,448]{2,1,0:T(8,128)S(1)}, f32[2,16,448,448]{2,3,1,0:T(8,128)}) fusion(pred[2,448,448]{1,2,0:T(8,128)(4,1)} %compare_and_fusion, bf16[2,448,16,32]{1,3,2,0:T(8,128)(2,1)} %copy.119, bf16[2,448,16,32]{1,3,2,0:T(8,128)(2,1)S(1)} %copy.118, bf16[2,448,64,1]{1,0,2,3:T(2,128)(2,1)S(1)} %bitcast.173), kind=kOutput, calls=%fused_computation.193 | convolution fusion | flops 851444160 | bytes 28098560 | tf_op jit(solution)/shard_map/vmap()/sub | solution.py:91
  276.4 12.1 %convert_bitcast_fusion = bf16[2,448,16,64]{1,3,2,0:T(8,128)(2,1)S(1)} fusion(f32[2,16,448,448]{2,3,1,0:T(8,128)} %get-tuple-element.37, f32[2,16,448]{2,1,0:T(8,128)S(1)} %get-tuple-element.36, bf16[2,448,64,1]{1,0,2,3:T(2,128)(2,1)S(1)} %bitcast.172), kind=kOutput, calls=%fused_computation.50 | convolution fusion | flops 835846144 | bytes 27697152 | tf_op jit(solution)/shard_map/vmap(hts,sd->thd)/dot_general | solution.py:93
  288.5 3.5 copy.124
  292.0 5.7 %reshape.686 = bf16[896,1024]{0,1:T(8,128)(2,1)} reshape(bf16[2,448,16,64]{1,0,3,2:T(2,128)(2,1)} %copy.124) | data formatting | bytes 3670016 | tf_op jit(solution)/shard_map/reshape | solution.py:290
  297.7 1.0 collective-permute-start.7
  299.1 40.9 %collective-permute-done.7 = bf16[896,1024]{0,1:T(8,128)(2,1)} collective-permute-done((bf16[896,1024]{0,1:T(8,128)(2,1)}, bf16[896,1024]{0,1:T(8,128)(2,1)}, u32[]{:S(2)}, u32[]{:S(2)}) %collective-permute-start.7) | collective-permute-done | bytes 1835040 | tf_op jit(solution)/shard_map/ppermute | solution.py:118
  340.0 2.0 fusion.110
  342.1 1.8 pad_maximum_fusion.2
  344.1 4.9 %gather_fusion = bf16[1024,128]{1,0:T(8,128)(2,1)S(1)} fusion(bf16[1,448,128]{2,1,0:T(8,128)(2,1)S(1)} %copy.138, s32[1024]{0:T(1024)S(1)} %fusion.84), kind=kCustom, calls=%fused_computation | custom fusion | bytes 532480 | tf_op jit(solution)/shard_map/vmap()/gather | solution.py:114
  349.0 1.5 fusion.107
  350.6 3.7 convolution_bitcast_fusion.3
  354.2 2.0 fusion.108
  356.3 1.6 fusion.20
  357.9 2.0 fusion.109
  359.9 1.5 convolution_bitcast_fusion
  361.5 1.7 fusion.25
  363.2 1.5 collective-permute-start.9
  364.7 0.9 broadcast_select_fusion.4
  365.6 1.5 convolution_bitcast_fusion.7
  367.2 1.6 fusion.23
  368.7 1.5 convolution_bitcast_fusion.4
  370.3 18.1 %collective-permute-done.9 = bf16[448,1136]{1,0:T(8,128)(2,1)S(1)} collective-permute-done((bf16[448,1136]{1,0:T(8,128)(2,1)S(1)}, bf16[448,1136]{1,0:T(8,128)(2,1)S(1)}, u32[]{:S(2)}, u32[]{:S(2)}) %collective-permute-start.9) | collective-permute-done | bytes 1017888 | tf_op jit(solution)/shard_map/ppermute | solution.py:118
  388.4 1.6 broadcast_select_fusion.3
  390.0 1.8 pad_maximum_fusion.1
  (128 shorter events, 5.7 us)
Async XLA Ops:
  7.2 1.4 copy-start.13
  7.2 1.7 copy-start.12
  7.2 1.9 copy-start.10
  7.2 207.3 %all-gather.5.cloned.1.call-start = ((), (), s32[]{:S(2)}) async-start(), calls=%async_computation | async-start | bytes 14598144 | tf_op jit(solution)/shard_map/all_gather | solution.py:196
  9.1 21.1 %collective-permute-start.2 = (bf16[288,1338]{1,0:T(8,128)(2,1)S(1)}, bf16[288,1338]{1,0:T(8,128)(2,1)S(1)}, u32[]{:S(2)}, u32[]{:S(2)}) collective-permute-start(bf16[288,1338]{1,0:T(8,128)(2,1)S(1)} %fusion.60), channel_id=1, source_target_pairs={{0,2},{2,0},{1,3},{3,1},{4,6},{6,4},{5,7},{7,5},{8,10},{10,8},{9,1... | collective-permute-start | bytes 2312072 | tf_op jit(solution)/shard_map/ppermute | solution.py:118
  30.6 1.5 copy-start.18
  30.6 1.5 copy-start.19
  32.0 318.6 %all-gather.7.cloned.1.call-start = ((), (), s32[]{:S(2)}) async-start(), calls=%async_computation.1 | async-start | bytes 10469376 | tf_op jit(solution)/shard_map/all_gather | solution.py:210
  32.0 3.4 copy-start
  69.4 4.2 %copy-start.24 = (s32[1,4]{1,0:T(1,128)S(1)}, s32[1,4]{1,0:T(1,128)}, u32[]{:S(2)}) copy-start(s32[1,4]{1,0:T(1,128)} %param.20) | copy-start | bytes 52
  69.4 4.2 %copy-start.26 = (s32[1,4]{1,0:T(1,128)S(1)}, s32[1,4]{1,0:T(1,128)}, u32[]{:S(2)}) copy-start(s32[1,4]{1,0:T(1,128)} %param.21) | copy-start | bytes 52
  69.4 4.5 %copy-start.5 = (bf16[256,2272]{0,1:T(8,128)(2,1)S(1)}, bf16[256,2272]{0,1:T(8,128)(2,1)}, u32[]{:S(2)}) copy-start(bf16[256,2272]{0,1:T(8,128)(2,1)} %param.17) | copy-start | bytes 3489796
  69.4 51.7 %copy-start.29 = (s32[16]{0:T(128)S(1)}, s32[16]{0:T(128)}, u32[]{:S(2)}) copy-start(s32[16]{0:T(128)} %param.23) | copy-start | bytes 196
  71.8 48.6 %collective-permute-start = (bf16[224,4608]{1,0:T(8,128)(2,1)}, bf16[224,4608]{1,0:T(8,128)(2,1)}, u32[]{:S(2)}, u32[]{:S(2)}) collective-permute-start(bf16[224,4608]{1,0:T(8,128)(2,1)} %copy.108), channel_id=1, source_target_pairs={{0,2},{2,0},{1,3},{3,1},{4,6},{6,4},{5,7},{7,5},{8,10},{10,8},{9,1... | collective-permute-start | bytes 6193160 | tf_op jit(solution)/shard_map/ppermute | solution.py:118
  73.7 46.3 %collective-permute-start.3 = (s32[1,8]{1,0:T(1,128)S(1)}, s32[1,8]{1,0:T(1,128)S(1)}, u32[]{:S(2)}, u32[]{:S(2)}) collective-permute-start(s32[1,8]{1,0:T(1,128)S(1)} %pad_add_fusion.1), channel_id=1, source_target_pairs={{0,2},{2,0},{1,3},{3,1},{4,6},{6,4},{5,7},{7,5},{8,10},{10,8},{9,1... | collective-permute-start | bytes 104 | tf_op jit(solution)/shard_map/ppermute | solution.py:118
  74.0 56.6 %collective-permute-start.5 = (bf16[256,1136]{0,1:T(8,128)(2,1)S(1)}, bf16[256,1136]{0,1:T(8,128)(2,1)S(1)}, u32[]{:S(2)}, u32[]{:S(2)}) collective-permute-start(bf16[256,1136]{0,1:T(8,128)(2,1)S(1)} %constant_dynamic-slice_fusion), channel_id=1, source_target_pairs={{0,2},{2,0},{1,3},{3,1},{4,6},{6,4},{5,7},{7,5},{8,10},{10,8},{9,1... | collective-permute-start | bytes 1744904 | tf_op jit(solution)/shard_map/ppermute | solution.py:118
  75.8 56.3 %copy-start.22 = (f32[32]{0:T(128)}, f32[32]{0:T(128)S(1)}, u32[]{:S(2)}) copy-start(f32[32]{0:T(128)S(1)} %multiply_exponential_fusion) | copy-start | bytes 388
  120.2 0.6 copy-start.20
  120.4 14.6 %collective-permute-start.1 = (bf16[224,4608]{1,0:T(8,128)(2,1)}, bf16[224,4608]{1,0:T(8,128)(2,1)}, u32[]{:S(2)}, u32[]{:S(2)}) collective-permute-start(bf16[224,4608]{1,0:T(8,128)(2,1)} %collective-permute-done), channel_id=1, source_target_pairs={{0,1},{1,0},{2,3},{3,2},{4,5},{5,4},{6,7},{7,6},{8,9},{9,8},{10,11... | collective-permute-start | bytes 6193160 | tf_op jit(solution)/shard_map/ppermute | solution.py:118
  120.9 11.2 %copy-start.16 = (f32[896]{0:T(1024)}, f32[896]{0:T(1024)S(1)}, u32[]{:S(2)}) copy-start(f32[896]{0:T(1024)S(1)} %convert_element_type.72) | copy-start | bytes 10756
  121.2 11.0 %copy-start.14 = (pred[896,8]{0,1:T(8,128)(4,1)}, pred[896,8]{0,1:T(8,128)(4,1)S(1)}, u32[]{:S(2)}) copy-start(pred[896,8]{0,1:T(8,128)(4,1)S(1)} %iota_compare_fusion.7) | copy-start | bytes 21508
  121.4 10.7 %copy-start.27 = (s32[8]{0:T(128)}, s32[8]{0:T(128)S(1)}, u32[]{:S(2)}) copy-start(s32[8]{0:T(128)S(1)} %select_reduce_fusion.3) | copy-start | bytes 100
  224.2 5.5 %copy-start.4 = (bf16[224,4608]{0,1:T(8,128)(2,1)S(1)}, bf16[224,4608]{0,1:T(8,128)(2,1)}, u32[]{:S(2)}) copy-start(bf16[224,4608]{0,1:T(8,128)(2,1)} %get-tuple-element.6) | copy-start | bytes 6193156
  224.2 28.1 %collective-permute-start.4 = (bf16[448,16]{0,1:T(8,128)(2,1)S(1)}, bf16[448,16]{0,1:T(8,128)(2,1)}, u32[]{:S(2)}, u32[]{:S(2)}) collective-permute-start(bf16[448,16]{0,1:T(8,128)(2,1)S(1)} %psum.7), channel_id=1, source_target_pairs={{0,2},{2,0},{1,3},{3,1},{4,6},{6,4},{5,7},{7,5},{8,10},{10,8},{9,1... | collective-permute-start | bytes 43016 | tf_op jit(solution)/shard_map/ppermute | solution.py:118
  229.7 19.5 %copy-start.17 = (f32[896]{0:T(1024)S(1)}, f32[896]{0:T(1024)}, u32[]{:S(2)}) copy-start(f32[896]{0:T(1024)} %copy-done.16) | copy-start | bytes 10756
  229.7 19.5 %copy-start.23 = (f32[32]{0:T(128)S(1)}, f32[32]{0:T(128)}, u32[]{:S(2)}) copy-start(f32[32]{0:T(128)} %copy-done.22) | copy-start | bytes 388
  229.8 20.0 %slice-start = ((bf16[16,16472]{1,0:T(8,128)(2,1)}), bf16[16,16384]{1,0:T(8,128)(2,1)S(1)}, s32[]{:S(2)}) async-start(bf16[16,16472]{1,0:T(8,128)(2,1)} %reshape.682), calls=%async_computation.2 | async-start | bytes 1048576 | tf_op jit(solution)/shard_map/slice | solution.py:24
  229.8 20.0 %copy-start.28 = (s32[8]{0:T(128)S(1)}, s32[8]{0:T(128)}, u32[]{:S(2)}) copy-start(s32[8]{0:T(128)} %copy-done.27) | copy-start | bytes 100
  249.2 2.2 copy-start.3
  249.2 4.0 copy-start.15
  253.1 2.8 copy-start.8
  253.1 2.8 copy-start.9
  259.7 16.7 %copy-start.11 = (bf16[2,448,64]{1,0,2:T(2,128)(2,1)S(1)}, bf16[2,448,64]{1,0,2:T(2,128)(2,1)}, u32[]{:S(2)}) copy-start(bf16[2,448,64]{1,0,2:T(2,128)(2,1)} %concatenate.56) | copy-start | bytes 344068
  292.0 6.7 %copy-start.30 = (s32[1,8]{1,0:T(1,128)S(1)}, s32[1,8]{1,0:T(1,128)}, u32[]{:S(2)}) copy-start(s32[1,8]{1,0:T(1,128)} %param.22) | copy-start | bytes 100
  292.0 6.8 %copy-start.21 = (s32[2,4]{1,0:T(2,128)S(1)}, s32[2,4]{1,0:T(2,128)}, u32[]{:S(2)}) copy-start(s32[2,4]{1,0:T(2,128)} %copy-done.20) | copy-start | bytes 100
  292.0 6.9 %copy-start.25 = (s32[1,4]{1,0:T(1,128)S(1)}, s32[1,4]{1,0:T(1,128)}, u32[]{:S(2)}) copy-start(s32[1,4]{1,0:T(1,128)} %param.20) | copy-start | bytes 52
  297.7 42.3 %collective-permute-start.7 = (bf16[896,1024]{0,1:T(8,128)(2,1)}, bf16[896,1024]{0,1:T(8,128)(2,1)}, u32[]{:S(2)}, u32[]{:S(2)}) collective-permute-start(bf16[896,1024]{0,1:T(8,128)(2,1)} %reshape.686), channel_id=1, source_target_pairs={{0,2},{2,0},{1,3},{3,1},{4,6},{6,4},{5,7},{7,5},{8,10},{10,8},{9,1... | collective-permute-start | bytes 5505032 | tf_op jit(solution)/shard_map/ppermute | solution.py:118
  299.0 55.2 %collective-permute-start.6 = (bf16[896,1024]{0,1:T(8,128)(2,1)}, bf16[896,1024]{0,1:T(8,128)(2,1)}, u32[]{:S(2)}, u32[]{:S(2)}) collective-permute-start(bf16[896,1024]{0,1:T(8,128)(2,1)} %reshape.686), channel_id=1, source_target_pairs={{0,1},{1,0},{2,3},{3,2},{4,5},{5,4},{6,7},{7,6},{8,9},{9,8},{10,11... | collective-permute-start | bytes 5505032 | tf_op jit(solution)/shard_map/ppermute | solution.py:118
  342.0 1.9 copy-start.1
  343.9 14.0 %collective-permute-start.8 = (bf16[896,1024]{0,1:T(8,128)(2,1)}, bf16[896,1024]{0,1:T(8,128)(2,1)}, u32[]{:S(2)}, u32[]{:S(2)}) collective-permute-start(bf16[896,1024]{0,1:T(8,128)(2,1)} %pad_maximum_fusion.2), channel_id=1, source_target_pairs={{0,1},{1,0},{2,3},{3,2},{4,5},{5,4},{6,7},{7,6},{8,9},{9,8},{10,11... | collective-permute-start | bytes 5505032 | tf_op jit(solution)/shard_map/ppermute | solution.py:118
  350.6 5.7 %copy-start.7 = (bf16[16,256,1136]{1,2,0:T(8,128)(2,1)S(1)}, bf16[16,256,1136]{1,2,0:T(8,128)(2,1)}, u32[]{:S(2)}) copy-start(bf16[16,256,1136]{1,2,0:T(8,128)(2,1)} %all-gather.7.cloned.1.call-done) | copy-start | bytes 27918340
  359.9 1.6 copy-start.2
  361.5 4.1 %copy-start.6 = (bf16[1,448,16,64]{1,3,2,0:T(8,128)(2,1)S(1)}, bf16[1,448,16,64]{1,3,2,0:T(8,128)(2,1)}, u32[]{:S(2)}) copy-start(bf16[1,448,16,64]{1,3,2,0:T(8,128)(2,1)} %get-tuple-element.10) | copy-start | bytes 2752516
  363.2 25.2 %collective-permute-start.9 = (bf16[448,1136]{1,0:T(8,128)(2,1)S(1)}, bf16[448,1136]{1,0:T(8,128)(2,1)S(1)}, u32[]{:S(2)}, u32[]{:S(2)}) collective-permute-start(bf16[448,1136]{1,0:T(8,128)(2,1)S(1)} %fusion.25), channel_id=1, source_target_pairs={{0,2},{2,0},{1,3},{3,1},{4,6},{6,4},{5,7},{7,5},{8,10},{10,8},{9,1... | collective-permute-start | bytes 3053576 | tf_op jit(solution)/shard_map/ppermute | solution.py:118
Sparse Core Ops, SparseCore 0:
  32.1 182.3 all-gather.4
  216.7 133.8 all-gather.6

commit v2 on v1

--- a/solution.py
+++ b/solution.py
@@ -208,7 +208,6 @@
     out_sent = half_of(output_weight, 1, 1 - side)
     out_pair = pair_join(out_kept[None], swap(out_sent, "dl")[None], side, 0)
     out_gathered = lax.all_gather(out_pair, "dh", axis=0, tiled=False)
-    heads_per_block = out_gathered.shape[0] * out_gathered.shape[1] // (2 * mp_count)
 
     normed_padded = pad_features(normed, shard_count, padded_rows)
     row_half = own_rows // mp_count
@@ -282,49 +281,54 @@
     local_heads = queries.shape[1]
     queries_grouped = queries.reshape(pair_groups, group_rows, local_heads, HEAD_SIZE)
     kv_grouped = kv_rot.reshape(pair_groups, group_rows, 2 * HEAD_SIZE)
-    context_grouped = jax.vmap(
-        lambda q_part, kv_part, idx_part: attend(
-            q_part, kv_part[:, :HEAD_SIZE], kv_part[:, HEAD_SIZE:], idx_part
-        )
-    )(queries_grouped, kv_grouped, index_grouped)
-    context = context_grouped.reshape(pair_rows, local_heads * HEAD_SIZE)
-
-    partner_context = swap(context, "dl")
-    partner_context = jnp.concatenate(
-        [partner_context[own_rows:], partner_context[:own_rows]], axis=0
-    )
-    block = context.shape[1]
-    if mp_count == 2:
-        other_mp = 1 - mp_index
-        pieces = [
-            (context, 2 * mp_index + side),
-            (swap(context, "mp"), 2 * other_mp + side),
-            (partner_context, 2 * mp_index + 1 - side),
-            (swap(partner_context, "mp"), 2 * other_mp + 1 - side),
-        ]
-    else:
-        stacked = lax.all_gather(jnp.stack([context, partner_context]), "mp", axis=0, tiled=False)
-        pieces = [
-            (stacked[m, which], 2 * m + jnp.where(which == 0, side, 1 - side))
+    def attend_groups(group_slice):
+        context_grouped = jax.vmap(
+            lambda q_part, kv_part, idx_part: attend(
+                q_part, kv_part[:, :HEAD_SIZE], kv_part[:, HEAD_SIZE:], idx_part
+            )
+        )(queries_grouped[group_slice], kv_grouped[group_slice], index_grouped[group_slice])
+        return context_grouped.reshape(own_rows, local_heads * HEAD_SIZE)
+
+    context_own = attend_groups(slice(0, group_count))
+    from_partner_for_partner_rows = swap(context_own, "dl")
+    context_partner_rows = attend_groups(slice(group_count, pair_groups))
+    from_partner_for_own_rows = swap(context_partner_rows, "dl")
+    block = context_own.shape[1]
+    blocks_per_quarter = out_gathered.shape[0] * out_gathered.shape[1] // (2 * mp_count)
+
+    def pieces_of(mine, theirs):
+        if mp_count == 2:
+            other_mp = 1 - mp_index
+            return [
+                (mine, 2 * mp_index + side),
+                (swap(mine, "mp"), 2 * other_mp + side),
+                (theirs, 2 * mp_index + 1 - side),
+                (swap(theirs, "mp"), 2 * other_mp + 1 - side),
+            ]
+        stacked = lax.all_gather(jnp.stack([mine, theirs]), "mp", axis=0, tiled=False)
+        return [
+            (stacked[m, which], 2 * m + (side if which == 0 else 1 - side))
             for which in range(2)
             for m in range(mp_count)
         ]
 
-    def project(row_start):
+    def project(pieces):
         total = None
         for piece, quarter in pieces:
-            rows = lax.dynamic_slice_in_dim(out_gathered, quarter * (heads_per_block // 2), heads_per_block // 2, 0)
+            rows = lax.dynamic_slice_in_dim(
+                out_gathered, quarter * (blocks_per_quarter // 2), blocks_per_quarter // 2, 0
+            )
             part = jnp.einsum(
                 "tabk,abkn->tn",
-                piece[row_start : row_start + own_rows].reshape((own_rows,) + rows.shape[:3]),
+                piece.reshape((own_rows,) + rows.shape[:3]),
                 rows,
                 preferred_element_type=jnp.float32,
             )
             total = part if total is None else total + part
         return total.astype(jnp.bfloat16)
 
-    received_out = swap(project(own_rows), "dl")
-    own_out = project(0)
+    received_out = swap(project(pieces_of(context_partner_rows, from_partner_for_partner_rows)), "dl")
+    own_out = project(pieces_of(context_own, from_partner_for_own_rows))
     attn_proj = pair_join(own_out, received_out, side, 1)
 
     cache_grouped = jax.vmap(

time: 404 us -> 421 us (1.042)
  matrix products: 69.1 us -> 94.1 us
  waiting for transfers between devices: 199 us -> 181 us
  other arithmetic: 26 us -> 38.4 us
    ppermute x10 -> x13, waiting for transfers between devices: 128 us -> 76.3 us  [swap(): return lax.ppermute(x, axis_name, [(0, 1), (1, 0)])]
    dot_general x8 -> x10, matrix products: 14.7 us -> 48.6 us  [the longest x8 34.6 us: project(): jnp.einsum('tabk,abkn->tn', piece.reshape((own_rows,) + rows.shape[:3]),...]
    all_gather x1, waiting for transfers between devices: 0.08 us -> 32.7 us  [shards(): out_gathered = lax.all_gather(out_pair, 'dh', axis=0, tiled=False)]
    sub x1 -> x0, matrix products: 16.7 us -> none  [attend(): weights = jnp.exp(scores - row_peak)]
    reduce_sum x0 -> x2, other arithmetic: none -> 16.5 us  [attend(): jnp.sum(weights, axis=-1, keepdims=True)]
    reshape x1 -> x8, local copies, waits for them, and re-layouts: 5.72 us -> 16.8 us  [the longest x6 13.2 us: project(): piece.reshape((own_rows,) + rows.shape[:3])]
    dot_general x1 -> x2, matrix products: 12.1 us -> 20 us  [attend(): jnp.einsum('hts,sd->thd', probs, values, preferred_element_type=jnp.float32)]
    slice x5 -> x2, local copies, waits for them, and re-layouts: 7.74 us -> 0.14 us  [the longest x1 0.14 us: attend_groups(): kv_grouped[group_slice]]
  transfers between devices with their start and end apart: 12 -> 15, of which waited for: 7 -> 6; matrix products, arithmetic and copies ran while one was open for 39% -> 46% of each run, Pallas kernels for 0% -> 0%
where the time goes in v2:
time: 421 us; the launch traced here: 415 us
  waiting for transfers between devices  181 us (43%)
  matrix products  94.1 us (22%)
  local copies, waits for them, and re-layouts  71.3 us (17%)
  other arithmetic  38.4 us (9%)
  between operations  14.9 us (4%)
  starting transfers between devices  12.5 us (3%)
    ppermute x13, waiting for transfers between devices, swap(): return lax.ppermute(x, axis_name, [(0, 1), (1, 0)])  76.3 us
    all_gather x1, waiting for transfers between devices, shards(): gathered = lax.all_gather(pair_block, 'dh', axis=0, tiled=False)  71.8 us
    dot_general x8, matrix products, project(): jnp.einsum('tabk,abkn->tn', piece.reshape((own_rows,) + rows.shape[:3]),...  34.6 us
    all_gather x1, waiting for transfers between devices, shards(): out_gathered = lax.all_gather(out_pair, 'dh', axis=0, tiled=False)  32.7 us
    dot_general x2, matrix products, attend(): jnp.einsum('hts,sd->thd', probs, values, preferred_element_type=jnp.float32)  20 us
    reshape x2, local copies, waits for them, and re-layouts, pad_features(): split = x.reshape(rows, shard_count, width // shard_count)  19.6 us
    dot_general x1, matrix products, shards(): jnp.dot(normed_pair, projection_block, preferred_element_type=jnp.float32)  19.3 us
    reduce_sum x2, other arithmetic, attend(): jnp.sum(weights, axis=-1, keepdims=True)  16.5 us
  transfers between devices with their start and end apart: 15, of which 6 were waited for; matrix products, arithmetic and copies ran while one was open for 46% of the time, Pallas kernels for 0%

profile of v2, /device:TPU:0, one launch (start us, length us, event | category | flops | bytes accessed | tf_op | source)
XLA Modules:
  0.0 415.4 jit_solution(11704267071741217054)
XLA Ops:
  7.2 1.4 constant_dynamic-slice_fusion.2
  9.1 3.0 collective-permute-start.2
  12.4 17.8 %collective-permute-done.2 = bf16[288,1338]{1,0:T(8,128)(2,1)S(1)} collective-permute-done((bf16[288,1338]{1,0:T(8,128)(2,1)S(1)}, bf16[288,1338]{1,0:T(8,128)(2,1)S(1)}, u32[]{:S(2)}, u32[]{:S(2)}) %collective-permute-start.2) | collective-permute-done | bytes 770720 | tf_op jit(solution)/shard_map/ppermute | solution.py:118
  30.6 1.3 pad_maximum_fusion.1
  32.1 3.0 convert_reduce_fusion
  35.4 1.2 fusion.6
  36.7 4.3 %fusion.9 = bf16[448,4544]{1,0:T(8,128)(2,1)} fusion(bf16[448,4544]{1,0:T(8,128)(2,1)S(1)} %copy-done, f32[4544]{0:T(1024)S(1)} %convert_element_type.82, f32[4544]{0:T(1024)S(1)} %convert_element_type.81, f32[448]{0:T(512)S(1)} %add_rsqrt_fusion, f32[448]{0:T(512)S(1)} %broadcast_multiply_fusion), kind=kLoop, calls=%fused_computation.18 | loop fusion | flops 12214272 | bytes 8182784 | tf_op jit(solution)/shard_map/convert_element_type | solution.py:47
  41.0 11.2 %reshape.869 = bf16[448,16,284]{2,1,0:T(8,128)(2,1)} reshape(bf16[448,4544]{1,0:T(8,128)(2,1)} %fusion.9) | data formatting | bytes 8142848 | tf_op jit(solution)/shard_map/reshape | solution.py:30
  52.2 8.4 %copy.127 = bf16[448,16,284]{0,2,1:T(8,128)(2,1)} copy(bf16[448,16,284]{2,1,0:T(8,128)(2,1)} %reshape.869) | data formatting | bytes 8142848 | tf_op jit(solution)/shard_map/reshape | solution.py:30
  60.5 5.3 %pad.34 = bf16[448,16,288]{0,2,1:T(8,128)(2,1)} pad(bf16[448,16,284]{0,2,1:T(8,128)(2,1)} %copy.127, bf16[]{:T(256)} %constant.32.clone.1), padding=0_0x0_0x0_4 | pad | bytes 8200194 | tf_op jit(solution)/shard_map/jit(_pad)/pad | solution.py:31
  65.8 3.2 constant_dynamic-slice_fusion.3
  69.1 2.4 copy.89
  71.5 1.7 collective-permute-start
  73.6 1.8 collective-permute-start.5
  75.6 44.0 %collective-permute-done.3 = s32[1,8]{1,0:T(1,128)S(1)} collective-permute-done((s32[1,8]{1,0:T(1,128)S(1)}, s32[1,8]{1,0:T(1,128)S(1)}, u32[]{:S(2)}, u32[]{:S(2)}) %collective-permute-start.3) | collective-permute-done | bytes 64 | tf_op jit(solution)/shard_map/ppermute | solution.py:118
  121.8 8.4 %collective-permute-done.5 = bf16[256,1136]{0,1:T(8,128)(2,1)S(1)} collective-permute-done((bf16[256,1136]{0,1:T(8,128)(2,1)S(1)}, bf16[256,1136]{0,1:T(8,128)(2,1)S(1)}, u32[]{:S(2)}, u32[]{:S(2)}) %collective-permute-start.5) | collective-permute-done | bytes 581664 | tf_op jit(solution)/shard_map/ppermute | solution.py:118
  130.5 1.1 pad_maximum_fusion.2
  131.6 2.8 copy.90
  134.4 4.1 copy.91
  138.6 4.2 %broadcast_select_fusion.1 = (bf16[224,4608]{0,1:T(8,128)(2,1)}, bf16[224,4608]{0,1:T(8,128)(2,1)}) fusion(bf16[224,4608]{0,1:T(8,128)(2,1)S(1)} %copy.90, bf16[224,4608]{0,1:T(8,128)(2,1)} %copy.91, pred[]{:T(512)S(6)} %eq.146), kind=kLoop, calls=%fused_computation.52 | loop fusion | flops 2064384 | bytes 8257537 | tf_op jit(solution)/shard_map/jit(_where)/select_n | solution.py:138
  142.7 71.8 %all-gather.5.cloned.1.call-done = bf16[16,288,1338]{2,1,0:T(8,128)(2,1)} async-done(((bf16[2,288,1338]{2,1,0:T(8,128)(2,1)}), bf16[16,288,1338]{2,1,0:T(8,128)(2,1)}) %all-gather.5.cloned.1.call-update) | async-done | bytes 12331024 | tf_op jit(solution)/shard_map/all_gather | solution.py:196
  214.5 19.3 %fusion.10 = f32[896,1338]{0,1:T(8,128)S(1)} fusion(bf16[4608,1338]{1,0:T(8,128)(2,1)} %bitcast.196, bf16[224,4608]{0,1:T(8,128)(2,1)} %get-tuple-element.7, bf16[224,4608]{0,1:T(8,128)(2,1)} %get-tuple-element.6, bf16[448,4608]{0,1:T(8,128)(2,1)} %bitcast.189), kind=kOutput, calls=%fused_computation.19 | convolution fusion | flops 11073355776 | bytes 25383936 | tf_op jit(solution)/shard_map/dot_general | solution.py:273
  233.9 2.2 copy-done.1
  236.1 1.4 slice.132
  237.5 2.0 reshape_reshape.13
  240.0 2.6 fusion.57
  242.6 3.4 psum.7
  246.0 1.5 collective-permute-start.4
  247.6 1.3 slice.133
  248.9 1.8 reshape.826
  250.8 1.0 slice_bitcast_fusion
  252.8 2.8 slice_add_fusion
  255.5 0.6 subtract_convert_fusion
  256.1 6.9 %fusion.2 = (f32[16,448]{1,0:T(8,128)S(1)}, f32[448,448,16]{1,0,2:T(8,128)}) fusion(pred[448,448]{0,1:T(8,128)(4,1)S(1)} %fusion.72, bf16[896,16,32]{0,2,1:T(8,128)(2,1)S(1)} %get-tuple-element.8, bf16[896,16,32]{0,2,1:T(8,128)(2,1)S(1)} %get-tuple-element.9, bf16[1,448,128]{1,2,0:T(8,128)(2,1)S(1)} %get-tuple-element.20), kind=kOutput, calls=%fused_computation.9 | convolution fusion | flops 422503424 | bytes 15003648 | tf_op jit(solution)/shard_map/vmap(thd,sd->hts)/dot_general | solution.py:86
  263.0 8.3 %fusion = f32[16,448]{1,0:T(8,128)S(1)} fusion(f32[448,448,16]{1,0,2:T(8,128)} %get-tuple-element.33, f32[16,448]{1,0:T(8,128)S(1)} %get-tuple-element.32, pred[448,448]{0,1:T(8,128)(4,1)S(1)} %fusion.72), kind=kLoop, calls=%fused_computation.7 | loop fusion | flops 12837888 | bytes 13103104 | tf_op jit(solution)/shard_map/vmap()/reduce_sum | solution.py:92
  271.3 10.6 %fusion.47 = bf16[64,16,448]{2,0,1:T(8,128)(2,1)} fusion(f32[16,448]{1,0:T(8,128)S(1)} %fusion, f32[16,448]{1,0:T(8,128)S(1)} %get-tuple-element.32, f32[448,448,16]{1,0,2:T(8,128)} %get-tuple-element.33, pred[448,448]{0,1:T(8,128)(4,1)S(1)} %fusion.72, bf16[1,448,128]{1,2,0:T(8,128)(2,1)S(1)} %get-tuple-element.20), kind=kOutput, calls=%fused_computation.80 | convolution fusion | flops 427556864 | bytes 14123008 | tf_op jit(solution)/shard_map/vmap(hts,sd->thd)/dot_general | solution.py:93
  281.9 2.2 copy.101
  284.2 1.2 collective-permute-start.10
  285.3 7.1 %fusion.3 = (f32[16,448]{1,0:T(8,128)S(1)}, f32[448,448,16]{1,0,2:T(8,128)}) fusion(pred[448,448]{0,1:T(8,128)(4,1)S(1)} %fusion.71, bf16[896,16,32]{0,2,1:T(8,128)(2,1)S(1)} %get-tuple-element.9, bf16[896,16,32]{0,2,1:T(8,128)(2,1)S(1)} %get-tuple-element.8, bf16[1,448,128]{1,2,0:T(8,128)(2,1)S(1)} %get-tuple-element.21), kind=kOutput, calls=%fused_computation.10 | convolution fusion | flops 422503424 | bytes 15003648 | tf_op jit(solution)/shard_map/vmap(thd,sd->hts)/dot_general | solution.py:86
  292.5 8.3 %fusion.1 = f32[16,448]{1,0:T(8,128)S(1)} fusion(f32[448,448,16]{1,0,2:T(8,128)} %get-tuple-element.35, f32[16,448]{1,0:T(8,128)S(1)} %get-tuple-element.34, pred[448,448]{0,1:T(8,128)(4,1)S(1)} %fusion.71), kind=kLoop, calls=%fused_computation.8 | loop fusion | flops 12837888 | bytes 13103104 | tf_op jit(solution)/shard_map/vmap()/reduce_sum | solution.py:92
  300.7 9.4 %fusion.50 = bf16[64,16,448]{2,0,1:T(8,128)(2,1)S(1)} fusion(f32[16,448]{1,0:T(8,128)S(1)} %fusion.1, f32[16,448]{1,0:T(8,128)S(1)} %get-tuple-element.34, f32[448,448,16]{1,0,2:T(8,128)} %get-tuple-element.35, pred[448,448]{0,1:T(8,128)(4,1)S(1)} %fusion.71, bf16[1,448,128]{1,2,0:T(8,128)(2,1)S(1)} %get-tuple-element.21), kind=kOutput, calls=%fused_computation.81 | convolution fusion | flops 427556864 | bytes 14123008 | tf_op jit(solution)/shard_map/vmap(hts,sd->thd)/dot_general | solution.py:93
  310.1 1.3 copy.104
  311.4 0.9 collective-permute-start.7
  312.5 4.5 %gather_fusion = bf16[1024,128]{1,0:T(8,128)(2,1)S(1)} fusion(bf16[1,448,128]{2,1,0:T(8,128)(2,1)S(1)} %copy.113, s32[1024]{0:T(1024)S(1)} %fusion.101), kind=kCustom, calls=%fused_computation | custom fusion | bytes 532480 | tf_op jit(solution)/shard_map/vmap()/gather | solution.py:114
  317.0 0.9 broadcast_select_fusion.4
  317.9 0.5 collective-permute-start.6
  318.5 32.7 %all-gather.7.cloned.1.call-done = bf16[16,256,1136]{1,2,0:T(8,128)(2,1)} async-done(((bf16[2,256,1136]{1,2,0:T(8,128)(2,1)}), bf16[16,256,1136]{1,2,0:T(8,128)(2,1)}) %all-gather.7.cloned.1.call-update) | async-done | bytes 9306128 | tf_op jit(solution)/shard_map/all_gather | solution.py:210
  351.1 4.5 %convolution_bitcast_fusion.6 = f32[448,1136]{1,0:T(8,128)} fusion(bf16[448,2,2,256]{0,3,2,1:T(8,128)(2,1)S(1)} %bitcast.194, bf16[8,2,256,1136]{2,3,1,0:T(8,128)(2,1)} %bitcast.204, s32[]{:T(128)S(6)} %select_n.228), kind=kOutput, calls=%fused_computation.43 | convolution fusion | flops 1042284544 | bytes 5279748 | tf_op jit(solution)/shard_map/tabk,abkn->tn/dot_general | solution.py:321
  355.6 1.6 reshape.839
  357.2 3.7 reshape.838
  361.0 4.0 fusion.22
  365.0 4.4 %fusion.21 = f32[448,1136]{1,0:T(8,128)} fusion(f32[448,1136]{1,0:T(8,128)S(1)} %fusion.22, bf16[8,2,256,1136]{2,3,1,0:T(8,128)(2,1)} %bitcast.206, s32[]{:T(128)S(6)} %select_n.231, bf16[448,2,2,256]{3,2,1,0:T(2,128)(2,1)S(1)} %copy-done.5), kind=kOutput, calls=%fused_computation.34 | convolution fusion | flops 1042793472 | bytes 7315460 | tf_op jit(solution)/shard_map/tabk,abkn->tn/dot_general | solution.py:321
  369.4 2.8 reshape.840
  372.3 4.7 %fusion.27 = bf16[448,1136]{1,0:T(8,128)(2,1)} fusion(f32[448,1136]{1,0:T(8,128)} %fusion.21, bf16[8,2,256,1136]{2,3,1,0:T(8,128)(2,1)} %bitcast.207, s32[]{:T(128)S(6)} %select_n.232, bf16[448,2,2,256]{3,2,1,0:T(2,128)(2,1)S(1)} %reshape.840), kind=kOutput, calls=%fused_computation.46 | convolution fusion | flops 1043302400 | bytes 6326276 | tf_op jit(solution)/shard_map/tabk,abkn->tn/dot_general | solution.py:321
  377.0 1.5 collective-permute-start.12
  378.5 4.5 %convolution_bitcast_fusion.7 = f32[448,1136]{1,0:T(8,128)} fusion(bf16[448,2,2,256]{0,3,2,1:T(8,128)(2,1)S(1)} %bitcast.192, bf16[8,2,256,1136]{2,3,1,0:T(8,128)(2,1)} %bitcast.208, s32[]{:T(128)S(6)} %select_n.228), kind=kOutput, calls=%fused_computation.44 | convolution fusion | flops 1042284544 | bytes 5279748 | tf_op jit(solution)/shard_map/tabk,abkn->tn/dot_general | solution.py:321
  383.0 0.7 reshape.836
  383.7 3.8 reshape.831
  387.4 4.0 fusion.25
  391.4 4.4 %fusion.24 = f32[448,1136]{1,0:T(8,128)} fusion(f32[448,1136]{1,0:T(8,128)S(1)} %fusion.25, bf16[8,2,256,1136]{2,3,1,0:T(8,128)(2,1)} %bitcast.210, s32[]{:T(128)S(6)} %select_n.231, bf16[448,2,2,256]{3,2,1,0:T(2,128)(2,1)S(1)} %reshape.836), kind=kOutput, calls=%fused_computation.40 | convolution fusion | flops 1042793472 | bytes 7315460 | tf_op jit(solution)/shard_map/tabk,abkn->tn/dot_general | solution.py:321
  395.8 0.7 reshape.837
  396.5 6.0 %collective-permute-done.12 = bf16[448,1136]{1,0:T(8,128)(2,1)} collective-permute-done((bf16[448,1136]{1,0:T(8,128)(2,1)}, bf16[448,1136]{1,0:T(8,128)(2,1)}, u32[]{:S(2)}, u32[]{:S(2)}) %collective-permute-start.12) | collective-permute-done | bytes 1017888 | tf_op jit(solution)/shard_map/ppermute | solution.py:118
  402.4 4.0 broadcast_select_fusion.3
  406.5 1.8 pad_maximum_fusion
  (104 shorter events, 6.4 us)
Async XLA Ops:
  7.2 1.4 copy-start.10
  7.2 1.7 copy-start.9
  7.2 1.9 copy-start.8
  7.2 207.3 %all-gather.5.cloned.1.call-start = ((), (), s32[]{:S(2)}) async-start(), calls=%async_computation | async-start | bytes 14598144 | tf_op jit(solution)/shard_map/all_gather | solution.py:196
  9.1 21.1 %collective-permute-start.2 = (bf16[288,1338]{1,0:T(8,128)(2,1)S(1)}, bf16[288,1338]{1,0:T(8,128)(2,1)S(1)}, u32[]{:S(2)}, u32[]{:S(2)}) collective-permute-start(bf16[288,1338]{1,0:T(8,128)(2,1)S(1)} %fusion.78), channel_id=1, source_target_pairs={{0,2},{2,0},{1,3},{3,1},{4,6},{6,4},{5,7},{7,5},{8,10},{10,8},{9,1... | collective-permute-start | bytes 2312072 | tf_op jit(solution)/shard_map/ppermute | solution.py:118
  30.6 1.4 copy-start.11
  30.6 1.5 copy-start.12
  32.0 319.2 %all-gather.7.cloned.1.call-start = ((), (), s32[]{:S(2)}) async-start(), calls=%async_computation.1 | async-start | bytes 10469376 | tf_op jit(solution)/shard_map/all_gather | solution.py:210
  32.0 3.4 copy-start
  69.1 4.1 copy-start.13
  69.1 4.1 copy-start.14
  69.1 4.5 %copy-start.2 = (bf16[256,2272]{0,1:T(8,128)(2,1)S(1)}, bf16[256,2272]{0,1:T(8,128)(2,1)}, u32[]{:S(2)}) copy-start(bf16[256,2272]{0,1:T(8,128)(2,1)} %param.17) | copy-start | bytes 3489796
  69.1 6.3 %copy-start.15 = (s32[1,8]{1,0:T(1,128)S(1)}, s32[1,8]{1,0:T(1,128)}, u32[]{:S(2)}) copy-start(s32[1,8]{1,0:T(1,128)} %param.22) | copy-start | bytes 100
  69.1 51.5 %copy-start.16 = (s32[16]{0:T(128)S(1)}, s32[16]{0:T(128)}, u32[]{:S(2)}) copy-start(s32[16]{0:T(128)} %param.23) | copy-start | bytes 196
  71.5 58.7 %copy-start.3 = (bf16[256,2272]{0,1:T(8,128)(2,1)S(1)}, bf16[256,2272]{0,1:T(8,128)(2,1)}, u32[]{:S(2)}) copy-start(bf16[256,2272]{0,1:T(8,128)(2,1)} %param.17) | copy-start | bytes 3489796
  71.5 48.8 %collective-permute-start = (bf16[224,4608]{1,0:T(8,128)(2,1)}, bf16[224,4608]{1,0:T(8,128)(2,1)}, u32[]{:S(2)}, u32[]{:S(2)}) collective-permute-start(bf16[224,4608]{1,0:T(8,128)(2,1)} %copy.89), channel_id=1, source_target_pairs={{0,2},{2,0},{1,3},{3,1},{4,6},{6,4},{5,7},{7,5},{8,10},{10,8},{9,1... | collective-permute-start | bytes 6193160 | tf_op jit(solution)/shard_map/ppermute | solution.py:118
  73.3 46.3 %collective-permute-start.3 = (s32[1,8]{1,0:T(1,128)S(1)}, s32[1,8]{1,0:T(1,128)S(1)}, u32[]{:S(2)}, u32[]{:S(2)}) collective-permute-start(s32[1,8]{1,0:T(1,128)S(1)} %pad_add_fusion.1), channel_id=1, source_target_pairs={{0,2},{2,0},{1,3},{3,1},{4,6},{6,4},{5,7},{7,5},{8,10},{10,8},{9,1... | collective-permute-start | bytes 104 | tf_op jit(solution)/shard_map/ppermute | solution.py:118
  73.6 56.6 %collective-permute-start.5 = (bf16[256,1136]{0,1:T(8,128)(2,1)S(1)}, bf16[256,1136]{0,1:T(8,128)(2,1)S(1)}, u32[]{:S(2)}, u32[]{:S(2)}) collective-permute-start(bf16[256,1136]{0,1:T(8,128)(2,1)S(1)} %constant_dynamic-slice_fusion), channel_id=1, source_target_pairs={{0,2},{2,0},{1,3},{3,1},{4,6},{6,4},{5,7},{7,5},{8,10},{10,8},{9,1... | collective-permute-start | bytes 1744904 | tf_op jit(solution)/shard_map/ppermute | solution.py:118
  120.3 14.1 %collective-permute-start.1 = (bf16[224,4608]{1,0:T(8,128)(2,1)}, bf16[224,4608]{1,0:T(8,128)(2,1)}, u32[]{:S(2)}, u32[]{:S(2)}) collective-permute-start(bf16[224,4608]{1,0:T(8,128)(2,1)} %collective-permute-done), channel_id=1, source_target_pairs={{0,1},{1,0},{2,3},{3,2},{4,5},{5,4},{6,7},{7,6},{8,9},{9,8},{10,11... | collective-permute-start | bytes 6193160 | tf_op jit(solution)/shard_map/ppermute | solution.py:118
  233.9 2.2 copy-start.1
  246.0 6.6 %collective-permute-start.4 = (bf16[448,16]{0,1:T(8,128)(2,1)S(1)}, bf16[448,16]{0,1:T(8,128)(2,1)S(1)}, u32[]{:S(2)}, u32[]{:S(2)}) collective-permute-start(bf16[448,16]{0,1:T(8,128)(2,1)S(1)} %psum.7), channel_id=1, source_target_pairs={{0,2},{2,0},{1,3},{3,1},{4,6},{6,4},{5,7},{7,5},{8,10},{10,8},{9,1... | collective-permute-start | bytes 43016 | tf_op jit(solution)/shard_map/ppermute | solution.py:118
  252.7 18.6 %copy-start.6 = (bf16[1,448,128]{1,2,0:T(8,128)(2,1)}, bf16[1,448,128]{1,2,0:T(8,128)(2,1)S(1)}, u32[]{:S(2)}) copy-start(bf16[1,448,128]{1,2,0:T(8,128)(2,1)S(1)} %get-tuple-element.20) | copy-start | bytes 344068
  284.2 34.3 %collective-permute-start.10 = (bf16[448,1024]{1,0:T(8,128)(2,1)}, bf16[448,1024]{1,0:T(8,128)(2,1)S(1)}, u32[]{:S(2)}, u32[]{:S(2)}) collective-permute-start(bf16[448,1024]{1,0:T(8,128)(2,1)} %copy.101), channel_id=1, source_target_pairs={{0,2},{2,0},{1,3},{3,1},{4,6},{6,4},{5,7},{7,5},{8,10},{10,8},{9,1... | collective-permute-start | bytes 2752520 | tf_op jit(solution)/shard_map/ppermute | solution.py:118
  300.7 11.6 %copy-start.7 = (bf16[1,448,128]{1,2,0:T(8,128)(2,1)S(1)}, bf16[1,448,128]{1,2,0:T(8,128)(2,1)}, u32[]{:S(2)}) copy-start(bf16[1,448,128]{1,2,0:T(8,128)(2,1)} %copy-done.6) | copy-start | bytes 344068
  311.4 49.6 %collective-permute-start.7 = (bf16[448,1024]{1,0:T(8,128)(2,1)}, bf16[448,1024]{1,0:T(8,128)(2,1)S(1)}, u32[]{:S(2)}, u32[]{:S(2)}) collective-permute-start(bf16[448,1024]{1,0:T(8,128)(2,1)} %copy.104), channel_id=1, source_target_pairs={{0,2},{2,0},{1,3},{3,1},{4,6},{6,4},{5,7},{7,5},{8,10},{10,8},{9,1... | collective-permute-start | bytes 2752520 | tf_op jit(solution)/shard_map/ppermute | solution.py:118
  312.3 45.0 %collective-permute-start.9 = (bf16[448,1024]{1,0:T(8,128)(2,1)}, bf16[448,1024]{1,0:T(8,128)(2,1)}, u32[]{:S(2)}, u32[]{:S(2)}) collective-permute-start(bf16[448,1024]{1,0:T(8,128)(2,1)} %copy.104), channel_id=1, source_target_pairs={{0,1},{1,0},{2,3},{3,2},{4,5},{5,4},{6,7},{7,6},{8,9},{9,8},{10,11... | collective-permute-start | bytes 2752520 | tf_op jit(solution)/shard_map/ppermute | solution.py:118
  317.9 65.7 %collective-permute-start.6 = (bf16[448,1024]{1,0:T(8,128)(2,1)}, bf16[448,1024]{1,0:T(8,128)(2,1)}, u32[]{:S(2)}, u32[]{:S(2)}) collective-permute-start(bf16[448,1024]{1,0:T(8,128)(2,1)} %copy.101), channel_id=1, source_target_pairs={{0,1},{1,0},{2,3},{3,2},{4,5},{5,4},{6,7},{7,6},{8,9},{9,8},{10,11... | collective-permute-start | bytes 2752520 | tf_op jit(solution)/shard_map/ppermute | solution.py:118
  318.5 51.0 %collective-permute-start.11 = (bf16[448,1024]{1,0:T(8,128)(2,1)S(1)}, bf16[448,1024]{1,0:T(8,128)(2,1)}, u32[]{:S(2)}, u32[]{:S(2)}) collective-permute-start(bf16[448,1024]{1,0:T(8,128)(2,1)S(1)} %collective-permute-done.10), channel_id=1, source_target_pairs={{0,1},{1,0},{2,3},{3,2},{4,5},{5,4},{6,7},{7,6},{8,9},{9,8},{10,11... | collective-permute-start | bytes 2752520 | tf_op jit(solution)/shard_map/ppermute | solution.py:118
  361.0 4.1 copy-start.5
  361.0 34.8 %collective-permute-start.8 = (bf16[448,1024]{1,0:T(8,128)(2,1)S(1)}, bf16[448,1024]{1,0:T(8,128)(2,1)S(1)}, u32[]{:S(2)}, u32[]{:S(2)}) collective-permute-start(bf16[448,1024]{1,0:T(8,128)(2,1)S(1)} %collective-permute-done.7), channel_id=1, source_target_pairs={{0,1},{1,0},{2,3},{3,2},{4,5},{5,4},{6,7},{7,6},{8,9},{9,8},{10,11... | collective-permute-start | bytes 2752520 | tf_op jit(solution)/shard_map/ppermute | solution.py:118
  372.2 6.2 %copy-start.4 = (bf16[64,16,448]{2,0,1:T(8,128)(2,1)S(1)}, bf16[64,16,448]{2,0,1:T(8,128)(2,1)}, u32[]{:S(2)}) copy-start(bf16[64,16,448]{2,0,1:T(8,128)(2,1)} %fusion.47) | copy-start | bytes 2752516
  377.0 25.4 %collective-permute-start.12 = (bf16[448,1136]{1,0:T(8,128)(2,1)}, bf16[448,1136]{1,0:T(8,128)(2,1)}, u32[]{:S(2)}, u32[]{:S(2)}) collective-permute-start(bf16[448,1136]{1,0:T(8,128)(2,1)} %fusion.27), channel_id=1, source_target_pairs={{0,2},{2,0},{1,3},{3,1},{4,6},{6,4},{5,7},{7,5},{8,10},{10,8},{9,1... | collective-permute-start | bytes 3053576 | tf_op jit(solution)/shard_map/ppermute | solution.py:118
Sparse Core Ops, SparseCore 0:
  32.1 182.3 all-gather.4
  217.3 133.8 all-gather.6

commit v3 on v1

--- a/solution.py
+++ b/solution.py
@@ -138,6 +138,17 @@
         return [jnp.where(first, x, other), jnp.where(first, other, x)]
     stacked = lax.all_gather(x, "mp", axis=0, tiled=False)
     return [stacked[m] for m in range(mp_count)]
+
+
+def gather_by_permutes(x, axis_name, count):
+    by_shift = [x] + [
+        lax.ppermute(x, axis_name, [(i, (i + shift) % count) for i in range(count)])
+        for shift in range(1, count)
+    ]
+    reverse = jnp.stack(by_shift[::-1])
+    doubled = jnp.concatenate([reverse, reverse], axis=0)
+    start = (count - 1 - lax.axis_index(axis_name)) % count
+    return lax.dynamic_slice_in_dim(doubled, start, count, 0)
 
 
 def half_of(x, axis, which):
@@ -159,6 +170,7 @@
     prompt_page_table,
     adapter_storage,
     mp_count,
+    dh_count,
 ):
     side = lax.axis_index("dl")
     mp_index = lax.axis_index("mp")
@@ -207,7 +219,7 @@
     out_kept = half_of(output_weight, 1, side)
     out_sent = half_of(output_weight, 1, 1 - side)
     out_pair = pair_join(out_kept[None], swap(out_sent, "dl")[None], side, 0)
-    out_gathered = lax.all_gather(out_pair, "dh", axis=0, tiled=False)
+    out_gathered = gather_by_permutes(out_pair, "dh", dh_count)
     heads_per_block = out_gathered.shape[0] * out_gathered.shape[1] // (2 * mp_count)
 
     normed_padded = pad_features(normed, shard_count, padded_rows)
@@ -344,7 +356,7 @@
     )
     dp = ("dh", "dl")
     return jax.shard_map(
-        functools.partial(shards, mp_count=mp_count),
+        functools.partial(shards, mp_count=mp_count, dh_count=dp_count // 2),
         mesh=pair_mesh,
         in_specs=(
             P(dp, None),

time: 404 us -> 641 us (1.59)
  waiting for transfers between devices: 199 us -> 296 us
  starting transfers between devices: 11.1 us -> 94.7 us
  local copies, waits for them, and re-layouts: 75.3 us -> 98.6 us
  matrix products: 69.1 us -> 91.3 us
    ppermute x0 -> x7, waiting for transfers between devices: none -> 228 us  [gather_by_permutes(): lax.ppermute(x, axis_name, [(i, (i + shift) % count) for i in range(count)])]
    ppermute x0 -> x7, starting transfers between devices: none -> 85.2 us  [gather_by_permutes(): lax.ppermute(x, axis_name, [(i, (i + shift) % count) for i in range(count)])]
    all_gather x1, waiting for transfers between devices: 71.3 us -> 0.01 us  [shards(): gathered = lax.all_gather(pair_block, 'dh', axis=0, tiled=False)]
    ppermute x10, waiting for transfers between devices: 128 us -> 68 us  [swap(): return lax.ppermute(x, axis_name, [(0, 1), (1, 0)])]
    unnamed x65 -> x87, local copies, waits for them, and re-layouts: 2.24 us -> 25.2 us
    dot_general x8, matrix products: 14.7 us -> 26 us  [project(): jnp.einsum('tabk,abkn->tn', piece[row_start:row_start + own_rows].reshape...]
    sub x1, matrix products: 16.7 us -> 26.4 us  [attend(): weights = jnp.exp(scores - row_peak)]
  transfers between devices with their start and end apart: 12 -> 18, of which waited for: 7 -> 7; matrix products, arithmetic and copies ran while one was open for 39% -> 20% of each run, Pallas kernels for 0% -> 0%
where the time goes in v3:
time: 641 us; the launch traced here: 631 us
  waiting for transfers between devices  296 us (46%)
  local copies, waits for them, and re-layouts  98.6 us (15%)
  starting transfers between devices  94.7 us (15%)
  matrix products  91.3 us (14%)
  other arithmetic  30.9 us (5%)
  between operations  15.1 us (2%)
    ppermute x7, waiting for transfers between devices, gather_by_permutes(): lax.ppermute(x, axis_name, [(i, (i + shift) % count) for i in range(count)])  228 us
    ppermute x7, starting transfers between devices, gather_by_permutes(): lax.ppermute(x, axis_name, [(i, (i + shift) % count) for i in range(count)])  85.2 us
    ppermute x10, waiting for transfers between devices, swap(): return lax.ppermute(x, axis_name, [(0, 1), (1, 0)])  68 us
    sub x1, matrix products, attend(): weights = jnp.exp(scores - row_peak)  26.4 us
    dot_general x8, matrix products, project(): jnp.einsum('tabk,abkn->tn', piece[row_start:row_start + own_rows].reshape...  26 us
    unnamed x87, local copies, waits for them, and re-layouts  25.2 us
    reshape x2, local copies, waits for them, and re-layouts, pad_features(): split = x.reshape(rows, shard_count, width // shard_count)  19.4 us
    dot_general x1, matrix products, shards(): jnp.dot(normed_pair, projection_block, preferred_element_type=jnp.float32)  19.2 us
  transfers between devices with their start and end apart: 18, of which 7 were waited for; matrix products, arithmetic and copies ran while one was open for 20% of the time, Pallas kernels for 0%

profile of v3, /device:TPU:0, one launch (start us, length us, event | category | flops | bytes accessed | tf_op | source)
XLA Modules:
  0.0 631.1 jit_solution(15999081258609190008)
XLA Ops:
  9.3 1.3 constant_dynamic-slice_fusion.2
  10.7 3.0 collective-permute-start.2
  14.0 17.8 %collective-permute-done.2 = bf16[288,1338]{1,0:T(8,128)(2,1)S(1)} collective-permute-done((bf16[288,1338]{1,0:T(8,128)(2,1)S(1)}, bf16[288,1338]{1,0:T(8,128)(2,1)S(1)}, u32[]{:S(2)}, u32[]{:S(2)}) %collective-permute-start.2) | collective-permute-done | bytes 770720 | tf_op jit(solution)/shard_map/ppermute | solution.py:118
  32.2 1.4 pad_maximum_fusion.3
  33.7 1.7 collective-permute-start.3
  35.9 3.0 convert_reduce_fusion
  39.3 1.2 fusion.8
  40.5 4.3 fusion.11
  44.8 11.0 %reshape.719 = bf16[448,16,284]{2,1,0:T(8,128)(2,1)} reshape(bf16[448,4544]{1,0:T(8,128)(2,1)} %fusion.11) | data formatting | bytes 8142848 | tf_op jit(solution)/shard_map/reshape | solution.py:30
  55.8 8.4 %copy.153 = bf16[448,16,284]{0,2,1:T(8,128)(2,1)} copy(bf16[448,16,284]{2,1,0:T(8,128)(2,1)} %reshape.719) | data formatting | bytes 8142848 | tf_op jit(solution)/shard_map/reshape | solution.py:30
  64.2 5.2 pad.34
  69.4 3.2 constant_dynamic-slice_fusion.3
  72.7 2.4 copy.108
  75.0 1.7 collective-permute-start
  77.9 1.5 select_bitcast_fusion.3
  80.5 4.6 collective-permute-start.6
  88.9 2.0 collective-permute-start.12
  90.8 32.9 %collective-permute-done.6 = bf16[2,256,1136]{1,2,0:T(8,128)(2,1)} collective-permute-done((bf16[2,256,1136]{1,2,0:T(8,128)(2,1)}, bf16[2,256,1136]{1,2,0:T(8,128)(2,1)}, u32[]{:S(2)}, u32[]{:S(2)}) %collective-permute-start.6) | collective-permute-done | bytes 1163296 | tf_op jit(solution)/shard_map/ppermute | solution.py:145
  123.7 2.7 collective-permute-start.9
  126.4 2.3 bitcast_dynamic-update-slice_fusion.14
  128.7 20.9 %collective-permute-done.7 = bf16[2,256,1136]{1,2,0:T(8,128)(2,1)} collective-permute-done((bf16[2,256,1136]{1,2,0:T(8,128)(2,1)}, bf16[2,256,1136]{1,2,0:T(8,128)(2,1)}, u32[]{:S(2)}, u32[]{:S(2)}) %collective-permute-start.7) | collective-permute-done | bytes 1163296 | tf_op jit(solution)/shard_map/ppermute | solution.py:145
  149.9 2.4 bitcast_dynamic-update-slice_fusion.12
  152.2 21.4 %collective-permute-done.8 = bf16[2,256,1136]{1,2,0:T(8,128)(2,1)S(1)} collective-permute-done((bf16[2,256,1136]{1,2,0:T(8,128)(2,1)}, bf16[2,256,1136]{1,2,0:T(8,128)(2,1)S(1)}, u32[]{:S(2)}, u32[]{:S(2)}) %collective-permute-start.8) | collective-permute-done | bytes 1163296 | tf_op jit(solution)/shard_map/ppermute | solution.py:145
  173.6 75.4 %collective-permute-start.11 = (bf16[2,256,1136]{1,2,0:T(8,128)(2,1)}, bf16[2,256,1136]{1,2,0:T(8,128)(2,1)S(1)}, u32[]{:S(2)}, u32[]{:S(2)}) collective-permute-start(bf16[2,256,1136]{1,2,0:T(8,128)(2,1)} %pad_maximum_fusion.10), channel_id=1, source_target_pairs={{0,8},{4,12},{8,16},{12,20},{16,24},{20,28},{24,0},{28,4},{1,9},{5... | collective-permute-start | bytes 3489800 | tf_op jit(solution)/shard_map/ppermute | solution.py:145
  250.1 153.0 %collective-permute-done.9 = bf16[2,256,1136]{1,2,0:T(8,128)(2,1)S(1)} collective-permute-done((bf16[2,256,1136]{1,2,0:T(8,128)(2,1)}, bf16[2,256,1136]{1,2,0:T(8,128)(2,1)S(1)}, u32[]{:S(2)}, u32[]{:S(2)}) %collective-permute-start.9) | collective-permute-done | bytes 1163296 | tf_op jit(solution)/shard_map/ppermute | solution.py:145
  405.5 1.2 bitcast_dynamic-update-slice_fusion.4
  406.7 1.2 bitcast_dynamic-update-slice_fusion.2
  409.0 2.4 bitcast_dynamic-update-slice_fusion.15
  411.4 2.3 bitcast_dynamic-update-slice_fusion.13
  413.7 2.8 copy.109
  416.5 4.2 copy.110
  420.7 4.1 broadcast_select_fusion.1
  424.8 1.3 slice.119
  426.1 1.8 reshape_reshape.7
  427.9 1.3 slice.120
  429.3 2.7 reshape.682
  434.5 3.4 fusion.52
  437.9 4.4 psum.7
  442.3 1.8 collective-permute-start.4
  444.1 19.2 %fusion.12 = f32[896,1338]{0,1:T(8,128)S(1)} fusion(bf16[4608,1338]{1,0:T(8,128)(2,1)} %bitcast.184, bf16[224,4608]{0,1:T(8,128)(2,1)} %get-tuple-element.7, bf16[224,4608]{0,1:T(8,128)(2,1)S(1)} %copy-done.15, bf16[448,4608]{0,1:T(8,128)(2,1)} %bitcast.174), kind=kOutput, calls=%fused_computation.18 | convolution fusion | flops 11073355776 | bytes 25383936 | tf_op jit(solution)/shard_map/dot_general | solution.py:286
  463.8 1.6 copy-done.14
  466.6 2.9 slice_add_fusion
  469.5 1.5 subtract_convert_fusion
  471.0 3.5 concatenate.66
  476.8 26.4 %fusion.112 = (f32[2,16,448]{2,1,0:T(8,128)}, f32[2,16,448,448]{2,3,1,0:T(8,128)}) fusion(pred[2,448,448]{1,2,0:T(8,128)(4,1)} %compare_and_fusion, bf16[2,448,16,32]{1,3,2,0:T(8,128)(2,1)S(1)} %copy.119, bf16[2,448,16,32]{1,3,2,0:T(8,128)(2,1)} %copy.118, bf16[2,448,64,1]{1,0,2,3:T(2,128)(2,1)S(1)} %bitcast.188), kind=kOutput, calls=%fused_computation.209 | convolution fusion | flops 851444160 | bytes 28098560 | tf_op jit(solution)/shard_map/vmap()/sub | solution.py:91
  503.2 12.0 %convert_bitcast_fusion = bf16[2,448,16,64]{1,3,2,0:T(8,128)(2,1)S(1)} fusion(f32[2,16,448,448]{2,3,1,0:T(8,128)} %get-tuple-element.37, f32[2,16,448]{2,1,0:T(8,128)} %get-tuple-element.36, bf16[2,448,64,1]{1,0,2,3:T(2,128)(2,1)S(1)} %bitcast.187), kind=kOutput, calls=%fused_computation.50 | convolution fusion | flops 835846144 | bytes 27697152 | tf_op jit(solution)/shard_map/vmap(hts,sd->thd)/dot_general | solution.py:93
  515.2 3.5 copy.124
  518.7 5.7 reshape.686
  524.8 2.6 bitcast_dynamic-update-slice_fusion.11
  530.7 35.8 %collective-permute-done.14 = bf16[896,1024]{0,1:T(8,128)(2,1)S(1)} collective-permute-done((bf16[896,1024]{0,1:T(8,128)(2,1)}, bf16[896,1024]{0,1:T(8,128)(2,1)S(1)}, u32[]{:S(2)}, u32[]{:S(2)}) %collective-permute-start.14) | collective-permute-done | bytes 1835040 | tf_op jit(solution)/shard_map/ppermute | solution.py:118
  567.0 1.8 pad_maximum_fusion.2
  571.3 4.7 gather_fusion
  576.3 3.2 convolution_bitcast_fusion.3
  579.5 2.0 fusion.108
  581.5 3.3 fusion.20
  584.8 2.0 fusion.109
  586.9 3.3 convolution_bitcast_fusion
  590.2 3.2 fusion.25
  594.7 3.2 convolution_bitcast_fusion.7
  597.9 3.2 fusion.23
  601.2 3.2 convolution_bitcast_fusion.4
  604.4 14.3 %collective-permute-done.16 = bf16[448,1136]{1,0:T(8,128)(2,1)S(1)} collective-permute-done((bf16[448,1136]{1,0:T(8,128)(2,1)S(1)}, bf16[448,1136]{1,0:T(8,128)(2,1)S(1)}, u32[]{:S(2)}, u32[]{:S(2)}) %collective-permute-start.16) | collective-permute-done | bytes 1017888 | tf_op jit(solution)/shard_map/ppermute | solution.py:118
  618.7 3.4 broadcast_select_fusion.3
  622.1 1.8 pad_maximum_fusion.1
  (162 shorter events, 29.2 us)
Async XLA Ops:
  7.2 3.5 copy-start.25
  7.2 417.6 %all-gather.3.cloned.1.call-start = ((), (), s32[]{:S(2)}) async-start(), calls=%async_computation | async-start | bytes 14598144 | tf_op jit(solution)/shard_map/all_gather | solution.py:208
  10.7 21.1 %collective-permute-start.2 = (bf16[288,1338]{1,0:T(8,128)(2,1)S(1)}, bf16[288,1338]{1,0:T(8,128)(2,1)S(1)}, u32[]{:S(2)}, u32[]{:S(2)}) collective-permute-start(bf16[288,1338]{1,0:T(8,128)(2,1)S(1)} %fusion.60), channel_id=1, source_target_pairs={{0,2},{2,0},{1,3},{3,1},{4,6},{6,4},{5,7},{7,5},{8,10},{10,8},{9,1... | collective-permute-start | bytes 2312072 | tf_op jit(solution)/shard_map/ppermute | solution.py:118
  32.1 1.5 copy-start.31
  32.2 1.5 copy-start.32
  32.2 3.3 copy-start.16
  32.2 3.7 copy-start.26
  32.2 3.7 copy-start.27
  33.7 43.3 %collective-permute-start.3 = (s32[1,8]{1,0:T(1,128)S(1)}, s32[1,8]{1,0:T(1,128)S(1)}, u32[]{:S(2)}, u32[]{:S(2)}) collective-permute-start(s32[1,8]{1,0:T(1,128)S(1)} %pad_add_fusion.1), channel_id=1, source_target_pairs={{0,2},{2,0},{1,3},{3,1},{4,6},{6,4},{5,7},{7,5},{8,10},{10,8},{9,1... | collective-permute-start | bytes 104 | tf_op jit(solution)/shard_map/ppermute | solution.py:118
  35.5 42.4 %collective-permute-start.5 = (bf16[256,1136]{0,1:T(8,128)(2,1)S(1)}, bf16[256,1136]{0,1:T(8,128)(2,1)}, u32[]{:S(2)}, u32[]{:S(2)}) collective-permute-start(bf16[256,1136]{0,1:T(8,128)(2,1)S(1)} %constant_dynamic-slice_fusion), channel_id=1, source_target_pairs={{0,2},{2,0},{1,3},{3,1},{4,6},{6,4},{5,7},{7,5},{8,10},{10,8},{9,1... | collective-permute-start | bytes 1744904 | tf_op jit(solution)/shard_map/ppermute | solution.py:118
  35.9 3.4 copy-start
  72.6 4.1 copy-start.33
  75.0 330.4 %collective-permute-start = (bf16[224,4608]{1,0:T(8,128)(2,1)}, bf16[224,4608]{1,0:T(8,128)(2,1)}, u32[]{:S(2)}, u32[]{:S(2)}) collective-permute-start(bf16[224,4608]{1,0:T(8,128)(2,1)} %copy.108), channel_id=1, source_target_pairs={{0,2},{2,0},{1,3},{3,1},{4,6},{6,4},{5,7},{7,5},{8,10},{10,8},{9,1... | collective-permute-start | bytes 6193160 | tf_op jit(solution)/shard_map/ppermute | solution.py:118
  76.8 8.4 %copy-start.29 = (f32[32]{0:T(128)}, f32[32]{0:T(128)S(1)}, u32[]{:S(2)}) copy-start(f32[32]{0:T(128)S(1)} %multiply_exponential_fusion) | copy-start | bytes 388
  77.9 9.6 %copy-start.34 = (s32[16]{0:T(128)S(1)}, s32[16]{0:T(128)}, u32[]{:S(2)}) copy-start(s32[16]{0:T(128)} %param.23) | copy-start | bytes 196
  80.5 43.2 %collective-permute-start.6 = (bf16[2,256,1136]{1,2,0:T(8,128)(2,1)}, bf16[2,256,1136]{1,2,0:T(8,128)(2,1)}, u32[]{:S(2)}, u32[]{:S(2)}) collective-permute-start(bf16[2,256,1136]{1,2,0:T(8,128)(2,1)} %pad_maximum_fusion.10), channel_id=1, source_target_pairs={{0,28},{4,0},{8,4},{12,8},{16,12},{20,16},{24,20},{28,24},{1,29},{... | collective-permute-start | bytes 3489800 | tf_op jit(solution)/shard_map/ppermute | solution.py:145
  86.3 63.3 %collective-permute-start.7 = (bf16[2,256,1136]{1,2,0:T(8,128)(2,1)}, bf16[2,256,1136]{1,2,0:T(8,128)(2,1)}, u32[]{:S(2)}, u32[]{:S(2)}) collective-permute-start(bf16[2,256,1136]{1,2,0:T(8,128)(2,1)} %pad_maximum_fusion.10), channel_id=1, source_target_pairs={{0,24},{4,28},{8,0},{12,4},{16,8},{20,12},{24,16},{28,20},{1,25},{... | collective-permute-start | bytes 3489800 | tf_op jit(solution)/shard_map/ppermute | solution.py:145
  88.8 84.8 %collective-permute-start.8 = (bf16[2,256,1136]{1,2,0:T(8,128)(2,1)}, bf16[2,256,1136]{1,2,0:T(8,128)(2,1)S(1)}, u32[]{:S(2)}, u32[]{:S(2)}) collective-permute-start(bf16[2,256,1136]{1,2,0:T(8,128)(2,1)} %pad_maximum_fusion.10), channel_id=1, source_target_pairs={{0,20},{4,24},{8,28},{12,0},{16,4},{20,8},{24,12},{28,16},{1,21},{... | collective-permute-start | bytes 3489800 | tf_op jit(solution)/shard_map/ppermute | solution.py:145
  88.9 317.8 %collective-permute-start.12 = (bf16[2,256,1136]{1,2,0:T(8,128)(2,1)}, bf16[2,256,1136]{1,2,0:T(8,128)(2,1)S(1)}, u32[]{:S(2)}, u32[]{:S(2)}) collective-permute-start(bf16[2,256,1136]{1,2,0:T(8,128)(2,1)} %pad_maximum_fusion.10), channel_id=1, source_target_pairs={{0,4},{4,8},{8,12},{12,16},{16,20},{20,24},{24,28},{28,0},{1,5},{5... | collective-permute-start | bytes 3489800 | tf_op jit(solution)/shard_map/ppermute | solution.py:145
  123.7 279.3 %collective-permute-start.9 = (bf16[2,256,1136]{1,2,0:T(8,128)(2,1)}, bf16[2,256,1136]{1,2,0:T(8,128)(2,1)S(1)}, u32[]{:S(2)}, u32[]{:S(2)}) collective-permute-start(bf16[2,256,1136]{1,2,0:T(8,128)(2,1)} %pad_maximum_fusion.10), channel_id=1, source_target_pairs={{0,16},{4,20},{8,24},{12,28},{16,0},{20,4},{24,8},{28,12},{1,17},{... | collective-permute-start | bytes 3489800 | tf_op jit(solution)/shard_map/ppermute | solution.py:145
  149.6 254.7 %collective-permute-start.10 = (bf16[2,256,1136]{1,2,0:T(8,128)(2,1)}, bf16[2,256,1136]{1,2,0:T(8,128)(2,1)S(1)}, u32[]{:S(2)}, u32[]{:S(2)}) collective-permute-start(bf16[2,256,1136]{1,2,0:T(8,128)(2,1)} %pad_maximum_fusion.10), channel_id=1, source_target_pairs={{0,12},{4,16},{8,20},{12,24},{16,28},{20,0},{24,4},{28,8},{1,13},{... | collective-permute-start | bytes 3489800 | tf_op jit(solution)/shard_map/ppermute | solution.py:145
  173.6 230.7 %copy-start.5 = (bf16[2,256,1136]{1,2,0:T(8,128)(2,1)}, bf16[2,256,1136]{1,2,0:T(8,128)(2,1)S(1)}, u32[]{:S(2)}) copy-start(bf16[2,256,1136]{1,2,0:T(8,128)(2,1)S(1)} %collective-permute-done.8) | copy-start | bytes 3489796
  173.6 231.9 %collective-permute-start.11 = (bf16[2,256,1136]{1,2,0:T(8,128)(2,1)}, bf16[2,256,1136]{1,2,0:T(8,128)(2,1)S(1)}, u32[]{:S(2)}, u32[]{:S(2)}) collective-permute-start(bf16[2,256,1136]{1,2,0:T(8,128)(2,1)} %pad_maximum_fusion.10), channel_id=1, source_target_pairs={{0,8},{4,12},{8,16},{12,20},{16,24},{20,28},{24,0},{28,4},{1,9},{5... | collective-permute-start | bytes 3489800 | tf_op jit(solution)/shard_map/ppermute | solution.py:145
  403.1 2.4 copy-start.6
  404.3 2.4 copy-start.8
  405.5 11.0 %collective-permute-start.1 = (bf16[224,4608]{1,0:T(8,128)(2,1)}, bf16[224,4608]{1,0:T(8,128)(2,1)}, u32[]{:S(2)}, u32[]{:S(2)}) collective-permute-start(bf16[224,4608]{1,0:T(8,128)(2,1)} %collective-permute-done), channel_id=1, source_target_pairs={{0,1},{1,0},{2,3},{3,2},{4,5},{5,4},{6,7},{7,6},{8,9},{9,8},{10,11... | collective-permute-start | bytes 6193160 | tf_op jit(solution)/shard_map/ppermute | solution.py:118
  405.5 2.4 copy-start.10
  406.7 2.3 copy-start.3
  434.5 9.5 %copy-start.15 = (bf16[224,4608]{0,1:T(8,128)(2,1)S(1)}, bf16[224,4608]{0,1:T(8,128)(2,1)}, u32[]{:S(2)}) copy-start(bf16[224,4608]{0,1:T(8,128)(2,1)} %get-tuple-element.6) | copy-start | bytes 6193156
  442.3 23.5 %collective-permute-start.4 = (bf16[448,16]{0,1:T(8,128)(2,1)S(1)}, bf16[448,16]{0,1:T(8,128)(2,1)}, u32[]{:S(2)}, u32[]{:S(2)}) collective-permute-start(bf16[448,16]{0,1:T(8,128)(2,1)S(1)} %psum.7), channel_id=1, source_target_pairs={{0,2},{2,0},{1,3},{3,1},{4,6},{6,4},{5,7},{7,5},{8,10},{10,8},{9,1... | collective-permute-start | bytes 43016 | tf_op jit(solution)/shard_map/ppermute | solution.py:118
  444.1 19.2 %copy-start.30 = (f32[32]{0:T(128)S(1)}, f32[32]{0:T(128)}, u32[]{:S(2)}) copy-start(f32[32]{0:T(128)} %copy-done.29) | copy-start | bytes 388
  463.2 2.2 copy-start.14
  463.8 5.7 copy-start.19
  463.8 5.7 copy-start.21
  465.4 4.1 copy-start.17
  466.6 2.9 copy-start.23
  466.6 2.9 copy-start.24
  515.2 9.2 %copy-start.1 = (bf16[2,448,16,64]{1,3,2,0:T(8,128)(2,1)}, bf16[2,448,16,64]{1,3,2,0:T(8,128)(2,1)S(1)}, u32[]{:S(2)}) copy-start(bf16[2,448,16,64]{1,3,2,0:T(8,128)(2,1)S(1)} %convert_bitcast_fusion) | copy-start | bytes 5505028
  524.4 3.0 copy-start.7
  524.4 4.1 copy-start.9
  524.4 42.1 %collective-permute-start.14 = (bf16[896,1024]{0,1:T(8,128)(2,1)}, bf16[896,1024]{0,1:T(8,128)(2,1)S(1)}, u32[]{:S(2)}, u32[]{:S(2)}) collective-permute-start(bf16[896,1024]{0,1:T(8,128)(2,1)} %reshape.686), channel_id=1, source_target_pairs={{0,2},{2,0},{1,3},{3,1},{4,6},{6,4},{5,7},{7,5},{8,10},{10,8},{9,1... | collective-permute-start | bytes 5505032 | tf_op jit(solution)/shard_map/ppermute | solution.py:118
  527.4 2.2 copy-start.11
  530.7 48.8 %collective-permute-start.13 = (bf16[896,1024]{0,1:T(8,128)(2,1)}, bf16[896,1024]{0,1:T(8,128)(2,1)}, u32[]{:S(2)}, u32[]{:S(2)}) collective-permute-start(bf16[896,1024]{0,1:T(8,128)(2,1)} %reshape.686), channel_id=1, source_target_pairs={{0,1},{1,0},{2,3},{3,2},{4,5},{5,4},{6,7},{7,6},{8,9},{9,8},{10,11... | collective-permute-start | bytes 5505032 | tf_op jit(solution)/shard_map/ppermute | solution.py:118
  567.0 3.0 copy-start.12
  567.0 1.9 copy-start.4
  568.9 2.3 copy-start.20
  568.9 2.3 copy-start.22
  568.9 2.3 copy-start.18
  568.9 15.9 %collective-permute-start.15 = (bf16[896,1024]{0,1:T(8,128)(2,1)}, bf16[896,1024]{0,1:T(8,128)(2,1)}, u32[]{:S(2)}, u32[]{:S(2)}) collective-permute-start(bf16[896,1024]{0,1:T(8,128)(2,1)} %pad_maximum_fusion.2), channel_id=1, source_target_pairs={{0,1},{1,0},{2,3},{3,2},{4,5},{5,4},{6,7},{7,6},{8,9},{9,8},{10,11... | collective-permute-start | bytes 5505032 | tf_op jit(solution)/shard_map/ppermute | solution.py:118
  571.1 4.9 copy-start.2
  586.9 3.3 copy-start.13
  590.2 3.6 copy-start.28
  593.4 25.2 %collective-permute-start.16 = (bf16[448,1136]{1,0:T(8,128)(2,1)S(1)}, bf16[448,1136]{1,0:T(8,128)(2,1)S(1)}, u32[]{:S(2)}, u32[]{:S(2)}) collective-permute-start(bf16[448,1136]{1,0:T(8,128)(2,1)S(1)} %fusion.25), channel_id=1, source_target_pairs={{0,2},{2,0},{1,3},{3,1},{4,6},{6,4},{5,7},{7,5},{8,10},{10,8},{9,1... | collective-permute-start | bytes 3053576 | tf_op jit(solution)/shard_map/ppermute | solution.py:118
Sparse Core Ops, SparseCore 0:
  33.7 372.1 all-gather.2

commit v4 on v1

--- a/solution.py
+++ b/solution.py
@@ -310,20 +310,24 @@
             for m in range(mp_count)
         ]
 
-    def project(row_start):
+    def project(row_start, row_count=own_rows):
         total = None
         for piece, quarter in pieces:
             rows = lax.dynamic_slice_in_dim(out_gathered, quarter * (heads_per_block // 2), heads_per_block // 2, 0)
             part = jnp.einsum(
                 "tabk,abkn->tn",
-                piece[row_start : row_start + own_rows].reshape((own_rows,) + rows.shape[:3]),
+                piece[row_start : row_start + row_count].reshape((row_count,) + rows.shape[:3]),
                 rows,
                 preferred_element_type=jnp.float32,
             )
             total = part if total is None else total + part
         return total.astype(jnp.bfloat16)
 
-    received_out = swap(project(own_rows), "dl")
+    half_rows = own_rows // 2
+    received_out = jnp.concatenate(
+        [swap(project(own_rows, half_rows), "dl"), swap(project(own_rows + half_rows, half_rows), "dl")],
+        axis=0,
+    )
     own_out = project(0)
     attn_proj = pair_join(own_out, received_out, side, 1)
 

time: 404 us -> 409 us (1.012)
  waiting for transfers between devices: 199 us -> 205 us
  local copies, waits for them, and re-layouts: 75.3 us -> 70.9 us
    all_gather x1, waiting for transfers between devices: 0.08 us -> 46.1 us  [shards(): out_gathered = lax.all_gather(out_pair, 'dh', axis=0, tiled=False)]
    ppermute x10 -> x11, waiting for transfers between devices: 128 us -> 91.3 us  [swap(): return lax.ppermute(x, axis_name, [(0, 1), (1, 0)])]
    dot_general x8 -> x12, matrix products: 14.7 us -> 16 us  [project(): jnp.einsum('tabk,abkn->tn', piece[row_start:row_start + row_count].reshap...]
    ppermute x10 -> x11, starting transfers between devices: 11 us -> 11.8 us  [swap(): return lax.ppermute(x, axis_name, [(0, 1), (1, 0)])]
  transfers between devices with their start and end apart: 12 -> 13, of which waited for: 7 -> 7; matrix products, arithmetic and copies ran while one was open for 39% -> 38% of each run, Pallas kernels for 0% -> 0%
where the time goes in v4:
time: 409 us; the launch traced here: 403 us
  waiting for transfers between devices  205 us (50%)
  matrix products  71.6 us (18%)
  local copies, waits for them, and re-layouts  70.9 us (17%)
  other arithmetic  25.3 us (6%)
  between operations  15 us (4%)
  starting transfers between devices  11.9 us (3%)
    ppermute x11, waiting for transfers between devices, swap(): return lax.ppermute(x, axis_name, [(0, 1), (1, 0)])  91.3 us
    all_gather x1, waiting for transfers between devices, shards(): gathered = lax.all_gather(pair_block, 'dh', axis=0, tiled=False)  67.8 us
    all_gather x1, waiting for transfers between devices, shards(): out_gathered = lax.all_gather(out_pair, 'dh', axis=0, tiled=False)  46.1 us
    reshape x2, local copies, waits for them, and re-layouts, pad_features(): split = x.reshape(rows, shard_count, width // shard_count)  20 us
    dot_general x1, matrix products, shards(): jnp.dot(normed_pair, projection_block, preferred_element_type=jnp.float32)  19.4 us
    sub x1, matrix products, attend(): weights = jnp.exp(scores - row_peak)  16.7 us
    dot_general x12, matrix products, project(): jnp.einsum('tabk,abkn->tn', piece[row_start:row_start + row_count].reshap...  16 us
    dot_general x1, matrix products, attend(): jnp.einsum('hts,sd->thd', probs, values, preferred_element_type=jnp.float32)  13.4 us
  transfers between devices with their start and end apart: 13, of which 7 were waited for; matrix products, arithmetic and copies ran while one was open for 38% of the time, Pallas kernels for 0%

profile of v4, /device:TPU:0, one launch (start us, length us, event | category | flops | bytes accessed | tf_op | source)
XLA Modules:
  0.0 403.3 jit_solution(4131323346803365604)
XLA Ops:
  7.2 1.4 constant_dynamic-slice_fusion.2
  9.1 3.0 collective-permute-start.2
  12.4 17.8 %collective-permute-done.2 = bf16[288,1338]{1,0:T(8,128)(2,1)S(1)} collective-permute-done((bf16[288,1338]{1,0:T(8,128)(2,1)S(1)}, bf16[288,1338]{1,0:T(8,128)(2,1)S(1)}, u32[]{:S(2)}, u32[]{:S(2)}) %collective-permute-start.2) | collective-permute-done | bytes 770720 | tf_op jit(solution)/shard_map/ppermute | solution.py:118
  30.6 1.4 pad_maximum_fusion.3
  32.1 3.0 convert_reduce_fusion
  35.5 1.2 fusion.8
  36.7 4.3 %fusion.11 = bf16[448,4544]{1,0:T(8,128)(2,1)} fusion(bf16[448,4544]{1,0:T(8,128)(2,1)S(1)} %copy-done.1, f32[4544]{0:T(1024)S(1)} %convert_element_type.72, f32[4544]{0:T(1024)S(1)} %convert_element_type.71, f32[448]{0:T(512)S(1)} %add_rsqrt_fusion, f32[448]{0:T(512)S(1)} %broadcast_multiply_fusion), kind=kLoop, calls=%fused_computation.17 | loop fusion | flops 12214272 | bytes 8182784 | tf_op jit(solution)/shard_map/convert_element_type | solution.py:47
  41.0 11.6 %reshape.738 = bf16[448,16,284]{2,1,0:T(8,128)(2,1)} reshape(bf16[448,4544]{1,0:T(8,128)(2,1)} %fusion.11) | data formatting | bytes 8142848 | tf_op jit(solution)/shard_map/reshape | solution.py:30
  52.5 8.4 %copy.191 = bf16[448,16,284]{0,2,1:T(8,128)(2,1)} copy(bf16[448,16,284]{2,1,0:T(8,128)(2,1)} %reshape.738) | data formatting | bytes 8142848 | tf_op jit(solution)/shard_map/reshape | solution.py:30
  60.9 5.2 %pad.34 = bf16[448,16,288]{0,2,1:T(8,128)(2,1)} pad(bf16[448,16,284]{0,2,1:T(8,128)(2,1)} %copy.191, bf16[]{:T(256)} %constant.32.clone.1), padding=0_0x0_0x0_4 | pad | bytes 8200194 | tf_op jit(solution)/shard_map/jit(_pad)/pad | solution.py:31
  66.2 3.2 constant_dynamic-slice_fusion.3
  69.5 2.4 copy.134
  71.8 1.7 collective-permute-start
  74.0 1.8 collective-permute-start.5
  76.5 43.4 %collective-permute-done.3 = s32[1,8]{1,0:T(1,128)S(1)} collective-permute-done((s32[1,8]{1,0:T(1,128)S(1)}, s32[1,8]{1,0:T(1,128)S(1)}, u32[]{:S(2)}, u32[]{:S(2)}) %collective-permute-start.3) | collective-permute-done | bytes 64 | tf_op jit(solution)/shard_map/ppermute | solution.py:118
  120.4 10.2 %collective-permute-done.5 = bf16[256,1136]{0,1:T(8,128)(2,1)S(1)} collective-permute-done((bf16[256,1136]{0,1:T(8,128)(2,1)S(1)}, bf16[256,1136]{0,1:T(8,128)(2,1)S(1)}, u32[]{:S(2)}, u32[]{:S(2)}) %collective-permute-start.5) | collective-permute-done | bytes 581664 | tf_op jit(solution)/shard_map/ppermute | solution.py:118
  130.9 1.2 pad_maximum_fusion.10
  133.3 1.2 multiply_cosine_fusion
  134.5 1.2 compare_and_fusion
  135.7 2.8 copy.135
  138.4 4.2 %copy.136 = bf16[224,4608]{0,1:T(8,128)(2,1)} copy(bf16[224,4608]{1,0:T(8,128)(2,1)} %collective-permute-done.1) | data formatting | bytes 4128768 | tf_op jit(solution)/shard_map/ppermute | solution.py:118
  142.6 4.1 %broadcast_select_fusion.1 = (bf16[224,4608]{0,1:T(8,128)(2,1)}, bf16[224,4608]{0,1:T(8,128)(2,1)}) fusion(bf16[224,4608]{0,1:T(8,128)(2,1)S(1)} %copy.135, bf16[224,4608]{0,1:T(8,128)(2,1)} %copy.136, pred[]{:T(512)S(6)} %eq.121), kind=kLoop, calls=%fused_computation.56 | loop fusion | flops 2064384 | bytes 8257537 | tf_op jit(solution)/shard_map/jit(_where)/select_n | solution.py:138
  146.7 67.8 %all-gather.5.cloned.1.call-done = bf16[16,288,1338]{2,1,0:T(8,128)(2,1)} async-done(((bf16[2,288,1338]{2,1,0:T(8,128)(2,1)}), bf16[16,288,1338]{2,1,0:T(8,128)(2,1)}) %all-gather.5.cloned.1.call-update) | async-done | bytes 12331024 | tf_op jit(solution)/shard_map/all_gather | solution.py:196
  214.5 1.3 slice.140
  215.9 1.8 reshape_reshape.7
  218.2 2.6 fusion.60
  220.8 3.4 psum.7
  224.2 1.5 collective-permute-start.4
  225.8 1.3 slice.141
  227.1 2.6 reshape.692
  229.8 19.4 %fusion.12 = f32[896,1338]{0,1:T(8,128)S(1)} fusion(bf16[4608,1338]{1,0:T(8,128)(2,1)} %bitcast.209, bf16[224,4608]{0,1:T(8,128)(2,1)} %get-tuple-element.7, bf16[224,4608]{0,1:T(8,128)(2,1)S(1)} %copy-done.3, bf16[448,4608]{0,1:T(8,128)(2,1)} %bitcast.195), kind=kOutput, calls=%fused_computation.18 | convolution fusion | flops 11073355776 | bytes 25383936 | tf_op jit(solution)/shard_map/dot_general | solution.py:274
  250.0 1.3 copy-done.2
  251.7 0.8 pad_maximum_fusion.12
  252.5 2.8 slice_add_fusion
  255.9 0.9 concatenate.65
  257.0 0.9 concatenate.66
  257.8 1.2 copy.145
  259.0 16.7 %fusion.125 = (f32[2,16,448]{2,1,0:T(8,128)S(1)}, f32[2,16,448,448]{2,3,1,0:T(8,128)}) fusion(pred[2,448,448]{1,2,0:T(8,128)(4,1)} %compare_and_fusion, bf16[2,448,16,32]{1,3,2,0:T(8,128)(2,1)} %copy.145, bf16[2,448,16,32]{1,3,2,0:T(8,128)(2,1)S(1)} %copy.144, bf16[2,448,64,1]{1,0,2,3:T(2,128)(2,1)S(1)} %bitcast.213), kind=kOutput, calls=%fused_computation.212 | convolution fusion | flops 851444160 | bytes 28098560 | tf_op jit(solution)/shard_map/vmap()/sub | solution.py:91
  275.7 13.4 %convert_bitcast_fusion = bf16[2,448,16,64]{1,3,2,0:T(8,128)(2,1)} fusion(f32[2,16,448,448]{2,3,1,0:T(8,128)} %get-tuple-element.39, f32[2,16,448]{2,1,0:T(8,128)S(1)} %get-tuple-element.38, bf16[2,448,64,1]{1,0,2,3:T(2,128)(2,1)S(1)} %bitcast.212), kind=kOutput, calls=%fused_computation.58 | convolution fusion | flops 835846144 | bytes 27697152 | tf_op jit(solution)/shard_map/vmap(hts,sd->thd)/dot_general | solution.py:93
  289.1 3.8 copy.150
  292.9 2.6 reshape.696
  295.4 1.0 collective-permute-start.7
  296.9 4.9 %gather_fusion = bf16[1024,128]{1,0:T(8,128)(2,1)S(1)} fusion(bf16[1,448,128]{2,1,0:T(8,128)(2,1)S(1)} %copy.173, s32[1024]{0:T(1024)S(1)} %fusion.92), kind=kCustom, calls=%fused_computation | custom fusion | bytes 532480 | tf_op jit(solution)/shard_map/vmap()/gather | solution.py:114
  301.9 0.9 broadcast_select_fusion.4
  302.8 1.7 fusion.121
  304.5 46.1 %all-gather.7.cloned.1.call-done = bf16[16,256,1136]{1,2,0:T(8,128)(2,1)} async-done(((bf16[2,256,1136]{1,2,0:T(8,128)(2,1)}), bf16[16,256,1136]{1,2,0:T(8,128)(2,1)}) %all-gather.7.cloned.1.call-update) | async-done | bytes 9306128 | tf_op jit(solution)/shard_map/all_gather | solution.py:210
  350.6 2.8 convolution_bitcast_fusion.7
  354.9 1.0 convolution_bitcast_fusion.11
  356.1 1.5 convolution_bitcast_fusion.3
  357.7 1.3 slice.146
  359.0 1.7 fusion.120
  360.9 0.9 fusion.24
  361.9 0.9 fusion.27
  362.8 1.6 fusion.20
  364.8 1.0 convolution_bitcast_fusion.4
  365.8 1.0 convolution_bitcast_fusion.8
  366.8 1.0 fusion.28
  367.8 1.5 collective-permute-start.9
  369.3 1.2 fusion.29
  371.2 1.5 convolution_bitcast_fusion
  372.8 9.7 %collective-permute-done.9 = bf16[224,1136]{1,0:T(8,128)(2,1)S(1)} collective-permute-done((bf16[224,1136]{1,0:T(8,128)(2,1)S(1)}, bf16[224,1136]{1,0:T(8,128)(2,1)S(1)}, u32[]{:S(2)}, u32[]{:S(2)}) %collective-permute-start.9) | collective-permute-done | bytes 508960 | tf_op jit(solution)/shard_map/ppermute | solution.py:118
  382.5 10.2 %collective-permute-done.10 = bf16[224,1136]{1,0:T(8,128)(2,1)S(1)} collective-permute-done((bf16[224,1136]{1,0:T(8,128)(2,1)S(1)}, bf16[224,1136]{1,0:T(8,128)(2,1)S(1)}, u32[]{:S(2)}, u32[]{:S(2)}) %collective-permute-start.10) | collective-permute-done | bytes 508960 | tf_op jit(solution)/shard_map/ppermute | solution.py:118
  392.8 1.7 broadcast_select_fusion.3
  394.5 1.8 pad_maximum_fusion.1
  (135 shorter events, 10.9 us)
Async XLA Ops:
  7.2 1.4 copy-start.9
  7.2 1.7 copy-start.8
  7.2 1.9 copy-start.7
  7.2 207.3 %all-gather.5.cloned.1.call-start = ((), (), s32[]{:S(2)}) async-start(), calls=%async_computation | async-start | bytes 14598144 | tf_op jit(solution)/shard_map/all_gather | solution.py:196
  9.1 21.1 %collective-permute-start.2 = (bf16[288,1338]{1,0:T(8,128)(2,1)S(1)}, bf16[288,1338]{1,0:T(8,128)(2,1)S(1)}, u32[]{:S(2)}, u32[]{:S(2)}) collective-permute-start(bf16[288,1338]{1,0:T(8,128)(2,1)S(1)} %fusion.68), channel_id=1, source_target_pairs={{0,2},{2,0},{1,3},{3,1},{4,6},{6,4},{5,7},{7,5},{8,10},{10,8},{9,1... | collective-permute-start | bytes 2312072 | tf_op jit(solution)/shard_map/ppermute | solution.py:118
  30.6 1.5 copy-start.14
  30.6 1.5 copy-start.15
  32.0 318.6 %all-gather.7.cloned.1.call-start = ((), (), s32[]{:S(2)}) async-start(), calls=%async_computation.1 | async-start | bytes 10469376 | tf_op jit(solution)/shard_map/all_gather | solution.py:210
  32.0 3.4 copy-start.1
  69.4 4.2 %copy-start.18 = (s32[1,4]{1,0:T(1,128)S(1)}, s32[1,4]{1,0:T(1,128)}, u32[]{:S(2)}) copy-start(s32[1,4]{1,0:T(1,128)} %param.20) | copy-start | bytes 52
  69.4 4.1 %copy-start.21 = (s32[1,4]{1,0:T(1,128)S(1)}, s32[1,4]{1,0:T(1,128)}, u32[]{:S(2)}) copy-start(s32[1,4]{1,0:T(1,128)} %param.21) | copy-start | bytes 52
  69.4 4.5 %copy-start.4 = (bf16[256,2272]{0,1:T(8,128)(2,1)S(1)}, bf16[256,2272]{0,1:T(8,128)(2,1)}, u32[]{:S(2)}) copy-start(bf16[256,2272]{0,1:T(8,128)(2,1)} %param.17) | copy-start | bytes 3489796
  69.4 6.3 %copy-start.26 = (s32[1,8]{1,0:T(1,128)S(1)}, s32[1,8]{1,0:T(1,128)}, u32[]{:S(2)}) copy-start(s32[1,8]{1,0:T(1,128)} %param.22) | copy-start | bytes 100
  71.8 48.5 %collective-permute-start = (bf16[224,4608]{1,0:T(8,128)(2,1)}, bf16[224,4608]{1,0:T(8,128)(2,1)}, u32[]{:S(2)}, u32[]{:S(2)}) collective-permute-start(bf16[224,4608]{1,0:T(8,128)(2,1)} %copy.134), channel_id=1, source_target_pairs={{0,2},{2,0},{1,3},{3,1},{4,6},{6,4},{5,7},{7,5},{8,10},{10,8},{9,1... | collective-permute-start | bytes 6193160 | tf_op jit(solution)/shard_map/ppermute | solution.py:118
  73.6 46.3 %collective-permute-start.3 = (s32[1,8]{1,0:T(1,128)S(1)}, s32[1,8]{1,0:T(1,128)S(1)}, u32[]{:S(2)}, u32[]{:S(2)}) collective-permute-start(s32[1,8]{1,0:T(1,128)S(1)} %pad_add_fusion.1), channel_id=1, source_target_pairs={{0,2},{2,0},{1,3},{3,1},{4,6},{6,4},{5,7},{7,5},{8,10},{10,8},{9,1... | collective-permute-start | bytes 104 | tf_op jit(solution)/shard_map/ppermute | solution.py:118
  74.0 56.6 %collective-permute-start.5 = (bf16[256,1136]{0,1:T(8,128)(2,1)S(1)}, bf16[256,1136]{0,1:T(8,128)(2,1)S(1)}, u32[]{:S(2)}, u32[]{:S(2)}) collective-permute-start(bf16[256,1136]{0,1:T(8,128)(2,1)S(1)} %constant_dynamic-slice_fusion), channel_id=1, source_target_pairs={{0,2},{2,0},{1,3},{3,1},{4,6},{6,4},{5,7},{7,5},{8,10},{10,8},{9,1... | collective-permute-start | bytes 1744904 | tf_op jit(solution)/shard_map/ppermute | solution.py:118
  75.8 57.5 %copy-start.16 = (f32[32]{0:T(128)}, f32[32]{0:T(128)S(1)}, u32[]{:S(2)}) copy-start(f32[32]{0:T(128)S(1)} %multiply_exponential_fusion) | copy-start | bytes 388
  120.4 18.1 %collective-permute-start.1 = (bf16[224,4608]{1,0:T(8,128)(2,1)}, bf16[224,4608]{1,0:T(8,128)(2,1)}, u32[]{:S(2)}, u32[]{:S(2)}) collective-permute-start(bf16[224,4608]{1,0:T(8,128)(2,1)} %collective-permute-done), channel_id=1, source_target_pairs={{0,1},{1,0},{2,3},{3,2},{4,5},{5,4},{6,7},{7,6},{8,9},{9,8},{10,11... | collective-permute-start | bytes 6193160 | tf_op jit(solution)/shard_map/ppermute | solution.py:118
  130.9 1.6 copy-start.27
  132.2 2.3 copy-start.12
  132.5 2.0 copy-start.10
  132.7 1.8 copy-start.24
  224.2 5.5 %copy-start.3 = (bf16[224,4608]{0,1:T(8,128)(2,1)S(1)}, bf16[224,4608]{0,1:T(8,128)(2,1)}, u32[]{:S(2)}) copy-start(bf16[224,4608]{0,1:T(8,128)(2,1)} %get-tuple-element.6) | copy-start | bytes 6193156
  224.2 27.4 %collective-permute-start.4 = (bf16[448,16]{0,1:T(8,128)(2,1)S(1)}, bf16[448,16]{0,1:T(8,128)(2,1)}, u32[]{:S(2)}, u32[]{:S(2)}) collective-permute-start(bf16[448,16]{0,1:T(8,128)(2,1)S(1)} %psum.7), channel_id=1, source_target_pairs={{0,2},{2,0},{1,3},{3,1},{4,6},{6,4},{5,7},{7,5},{8,10},{10,8},{9,1... | collective-permute-start | bytes 43016 | tf_op jit(solution)/shard_map/ppermute | solution.py:118
  229.7 19.5 %copy-start.13 = (f32[896]{0:T(1024)S(1)}, f32[896]{0:T(1024)}, u32[]{:S(2)}) copy-start(f32[896]{0:T(1024)} %copy-done.12) | copy-start | bytes 10756
  229.7 19.5 %copy-start.17 = (f32[32]{0:T(128)S(1)}, f32[32]{0:T(128)}, u32[]{:S(2)}) copy-start(f32[32]{0:T(128)} %copy-done.16) | copy-start | bytes 388
  229.7 20.0 %slice-start.1 = ((bf16[16,16472]{1,0:T(8,128)(2,1)}), bf16[16,16384]{1,0:T(8,128)(2,1)S(1)}, s32[]{:S(2)}) async-start(bf16[16,16472]{1,0:T(8,128)(2,1)} %reshape.692), calls=%async_computation.3 | async-start | bytes 1048576 | tf_op jit(solution)/shard_map/slice | solution.py:24
  229.7 20.0 %copy-start.25 = (s32[8]{0:T(128)S(1)}, s32[8]{0:T(128)}, u32[]{:S(2)}) copy-start(s32[8]{0:T(128)} %copy-done.24) | copy-start | bytes 100
  249.2 2.2 copy-start.2
  249.2 3.3 copy-start.11
  252.5 2.8 copy-start.5
  252.5 2.8 copy-start.6
  292.8 3.6 copy-start.19
  292.8 3.6 copy-start.22
  292.8 3.6 copy-start.23
  292.8 3.7 copy-start.20
  295.4 57.9 %collective-permute-start.7 = (bf16[896,1024]{0,1:T(8,128)(2,1)}, bf16[896,1024]{0,1:T(8,128)(2,1)S(1)}, u32[]{:S(2)}, u32[]{:S(2)}) collective-permute-start(bf16[896,1024]{0,1:T(8,128)(2,1)} %reshape.696), channel_id=1, source_target_pairs={{0,2},{2,0},{1,3},{3,1},{4,6},{6,4},{5,7},{7,5},{8,10},{10,8},{9,1... | collective-permute-start | bytes 5505032 | tf_op jit(solution)/shard_map/ppermute | solution.py:118
  296.7 61.0 %collective-permute-start.6 = (bf16[896,1024]{0,1:T(8,128)(2,1)}, bf16[896,1024]{0,1:T(8,128)(2,1)}, u32[]{:S(2)}, u32[]{:S(2)}) collective-permute-start(bf16[896,1024]{0,1:T(8,128)(2,1)} %reshape.696), channel_id=1, source_target_pairs={{0,1},{1,0},{2,3},{3,2},{4,5},{5,4},{6,7},{7,6},{8,9},{9,8},{10,11... | collective-permute-start | bytes 5505032 | tf_op jit(solution)/shard_map/ppermute | solution.py:118
  350.6 4.3 %copy-start = (bf16[16,256,1136]{1,2,0:T(8,128)(2,1)S(1)}, bf16[16,256,1136]{1,2,0:T(8,128)(2,1)}, u32[]{:S(2)}) copy-start(bf16[16,256,1136]{1,2,0:T(8,128)(2,1)} %all-gather.7.cloned.1.call-done) | copy-start | bytes 27918340
  354.5 9.9 %collective-permute-start.8 = (bf16[896,1024]{0,1:T(8,128)(2,1)S(1)}, bf16[896,1024]{0,1:T(8,128)(2,1)S(1)}, u32[]{:S(2)}, u32[]{:S(2)}) collective-permute-start(bf16[896,1024]{0,1:T(8,128)(2,1)S(1)} %pad_maximum_fusion.2), channel_id=1, source_target_pairs={{0,1},{1,0},{2,3},{3,2},{4,5},{5,4},{6,7},{7,6},{8,9},{9,8},{10,11... | collective-permute-start | bytes 5505032 | tf_op jit(solution)/shard_map/ppermute | solution.py:118
  354.9 1.2 slice-start
  367.8 14.7 %collective-permute-start.9 = (bf16[224,1136]{1,0:T(8,128)(2,1)S(1)}, bf16[224,1136]{1,0:T(8,128)(2,1)S(1)}, u32[]{:S(2)}, u32[]{:S(2)}) collective-permute-start(bf16[224,1136]{1,0:T(8,128)(2,1)S(1)} %fusion.28), channel_id=1, source_target_pairs={{0,2},{2,0},{1,3},{3,1},{4,6},{6,4},{5,7},{7,5},{8,10},{10,8},{9,1... | collective-permute-start | bytes 1526792 | tf_op jit(solution)/shard_map/ppermute | solution.py:118
  370.5 22.2 %collective-permute-start.10 = (bf16[224,1136]{1,0:T(8,128)(2,1)S(1)}, bf16[224,1136]{1,0:T(8,128)(2,1)S(1)}, u32[]{:S(2)}, u32[]{:S(2)}) collective-permute-start(bf16[224,1136]{1,0:T(8,128)(2,1)S(1)} %fusion.29), channel_id=1, source_target_pairs={{0,2},{2,0},{1,3},{3,1},{4,6},{6,4},{5,7},{7,5},{8,10},{10,8},{9,1... | collective-permute-start | bytes 1526792 | tf_op jit(solution)/shard_map/ppermute | solution.py:118
Sparse Core Ops, SparseCore 0:
  32.1 182.3 all-gather.4
  216.7 133.8 all-gather.6
